TPU v7x, 128 devices: a whole 4x4x4 slice. The times are simulated.
128 devices in a mesh: section: 2 (over z_lo), cp: 16 (over y, z_hi, core), tp: 4 (over x).
Axes of the slice: x: 4, y: 4, z: 4 (z_hi: 2, z_lo: 2; z = z_hi * 2 + z_lo), core: 2. Of those that a mesh axis runs over, the one named last changes fastest.
Arguments:
- rollout_rows: bfloat16 [2048, 8192], P(('section', 'cp'), 'tp'), may hold values from -60 to 60
- lengths: int32 [2], replicated, may hold values from 1 to 1536, 2048 in all
- block_owner: int32 [32], replicated, may hold values from 0 to 31, each once
- norm_gain: float32 [2, 8192], P('section', 'tp'), may hold values from 0.1 to 1.9
- w_qkv: bfloat16 [2, 3, 8192, 8192], P('section', None, 'tp', 'cp'), may hold values from -1 to 1
- w_out: bfloat16 [2, 8192, 8192], P('section', 'cp', 'tp'), may hold values from -0.5 to 0.5
Outputs:
- scored: bfloat16 [2, 2048, 8192], P(None, ('section', 'cp'), 'tp')
Inputs may be any that keep to these rules, and one draw needn't show every extreme that they name: The 2 lengths sum to 2048; neither is over 1536. `block_owner`: every owner block appears once.
All inputs are finite; a program needn't handle non-finite values.
Results may differ from a plain program's by a relative error of at most 0.022.
Values may be sent and summed in bfloat16 or wider, within the bound.
No kernel may reach another device: no remote copies, remote signals or barrier semaphores. Data moves between devices by JAX's collectives and lax.ppermute only.
A program may use at most 128 MiB of HBM per device.

v0:
```python
import math

import jax
import jax.numpy as jnp
from jax import lax
from jax.sharding import PartitionSpec as P

D = 8192
HEAD = 128


def layout_position(layout_rows, tokens, tp_count):
    quarter = tokens // tp_count
    halfblock = quarter // 2
    owner_index = layout_rows // quarter
    second = layout_rows % quarter // halfblock
    offset = layout_rows % halfblock
    block_index = 2 * owner_index + second
    return block_index * halfblock + offset


def layout_row(position, tokens, tp_count):
    quarter = tokens // tp_count
    halfblock = quarter // 2
    block_index = position // halfblock
    offset = position % halfblock
    second = block_index % 2
    owner_index = block_index // 2
    return owner_index * quarter + second * halfblock + offset


def on_device(rollout_rows, lengths, block_owner, norm_gain, w_qkv, w_out):
    tp_count = lax.axis_size("tp")
    cp_count = lax.axis_size("cp")
    sections = lax.axis_size("section")
    own_rows, width_here = rollout_rows.shape
    blocks = sections * cp_count
    tokens = own_rows * blocks
    actor_rows = lax.all_gather(rollout_rows, ("section", "cp"), axis=0, tiled=True)
    layout_rows = jnp.arange(tokens, dtype=jnp.int32)
    position = layout_position(layout_rows, tokens, tp_count)
    source = block_owner[position // own_rows] * own_rows + position % own_rows
    rows_in = jnp.take(actor_rows, source, axis=0)
    seq_ends = jnp.cumsum(lengths)
    sequence = jnp.sum((position[:, None] >= seq_ends[None, :]).astype(jnp.int32), axis=1)
    squares = jnp.sum(jnp.square(rows_in.astype(jnp.float32)), axis=1)
    total_squares = lax.psum(squares, "tp")
    inverse_rms = lax.rsqrt(total_squares / D + 1e-05)
    normed = (rows_in.astype(jnp.float32) * norm_gain[0][None, :] * inverse_rms[:, None]).astype(
        jnp.bfloat16
    )
    qkv_weights = w_qkv[0]
    local_rows = tokens // tp_count
    halfblock = local_rows // 2
    heads_here = qkv_weights.shape[2] // HEAD
    first_local = lax.axis_index("tp") * local_rows
    query_pos = lax.dynamic_slice_in_dim(position, first_local, local_rows, 0).reshape(2, halfblock)
    query_seq = lax.dynamic_slice_in_dim(sequence, first_local, local_rows, 0).reshape(2, halfblock)
    inv_sqrt = 1.0 / math.sqrt(HEAD)
    initial = (
        jnp.full((2, heads_here, halfblock), -1e30, jnp.float32),
        jnp.zeros((2, heads_here, halfblock), jnp.float32),
        jnp.zeros((2, heads_here, halfblock, HEAD), jnp.float32),
    )
    projected = lax.psum_scatter(
        jnp.einsum("rd,kdc->rkc", normed, qkv_weights, preferred_element_type=jnp.float32),
        "tp",
        scatter_dimension=0,
        tiled=True,
    ).astype(jnp.bfloat16)
    query_blocks = projected[:, 0].reshape(2, halfblock, heads_here, HEAD)
    key_part = lax.all_gather(projected[:, 1], "tp", axis=0, tiled=True)
    value_part = lax.all_gather(projected[:, 2], "tp", axis=0, tiled=True)
    key_count = key_part.shape[0]
    key_heads = key_part.reshape(key_count, heads_here, HEAD)
    value_heads = value_part.reshape(key_count, heads_here, HEAD)
    results = []
    for sub_block in range(2):
        allowed = (query_seq[sub_block][:, None] == sequence[None, :]) & (
            position[None, :] <= query_pos[sub_block][:, None]
        )
        query_block = query_blocks[sub_block]

        def update(state_now):
            row_peak, row_total, weighted = state_now
            scores = (
                jnp.einsum(
                    "qhd,khd->hqk", query_block, key_heads, preferred_element_type=jnp.float32
                )
                * inv_sqrt
            )
            scores = jnp.where(allowed[None], scores, -1e30)
            new_peak = jnp.maximum(row_peak, jnp.max(scores, axis=2))
            weights_now = jnp.where(allowed[None], jnp.exp(scores - new_peak[:, :, None]), 0.0)
            row_total = jnp.sum(weights_now, axis=2)
            probabilities = weights_now.astype(jnp.bfloat16)
            weighted = jnp.einsum(
                "hqk,khd->hqd", probabilities, value_heads, preferred_element_type=jnp.float32
            )
            return (new_peak, row_total, weighted)

        def unchanged(state_now):
            return state_now

        results.append(
            lax.cond(
                jnp.any(allowed),
                update,
                unchanged,
                (initial[0][sub_block], initial[1][sub_block], initial[2][sub_block]),
            )
        )
    attended = (
        jnp.stack([results[0][2], results[1][2]])
        / jnp.stack([results[0][1], results[1][1]])[:, :, :, None]
    )
    attended = (
        attended.transpose(0, 2, 1, 3).reshape(local_rows, heads_here * HEAD).astype(jnp.bfloat16)
    )
    gathered = lax.all_gather(attended, "tp", axis=0, tiled=True)
    group_rows = sections * own_rows
    target_rows = jnp.arange(tokens, dtype=jnp.int32)
    cp_index = target_rows // group_rows
    owner_section = target_rows % group_rows // own_rows
    inner = target_rows % own_rows
    actor_block = owner_section * cp_count + cp_index
    block_ids = jnp.arange(blocks, dtype=jnp.int32)
    inverse_owner = jnp.sum(
        jnp.where(block_owner[None, :] == block_ids[:, None], block_ids[None, :], 0), axis=1
    )
    packed_pos = inverse_owner[actor_block] * own_rows + inner
    ordered = jnp.take(gathered, layout_row(packed_pos, tokens, tp_count), axis=0)
    out_weight = w_out[0]
    summed = lax.psum_scatter(
        jnp.dot(ordered, out_weight, preferred_element_type=jnp.float32).astype(jnp.bfloat16),
        "cp",
        scatter_dimension=0,
        tiled=True,
    )
    branch = summed.reshape(sections, own_rows, width_here)
    return lax.all_to_all(branch, "section", split_axis=0, concat_axis=0, tiled=True)


def solution(mesh):
    return jax.shard_map(
        on_device,
        mesh=mesh,
        in_specs=(
            P(("section", "cp"), "tp"),
            P(),
            P(),
            P("section", "tp"),
            P("section", None, "tp", "cp"),
            P("section", "cp", "tp"),
        ),
        out_specs=P(None, ("section", "cp"), "tp"),
        check_vma=False,
    )
```

profile of v0, /device:TPU:0, one launch (start us, length us, event | category | flops | bytes accessed | tf_op | source)
XLA Modules:
  0.0 519.2 jit_solution(15395411485198232677)
XLA Ops:
  6.5 0.7 all-gather.7.cloned.1.call-update
  7.3 0.1 compare_reduce_fusion
  7.4 0.1 compare_reduce_fusion.1
  7.6 0.1 compare_reduce_fusion.10
  7.7 0.1 compare_reduce_fusion.11
  7.8 0.1 compare_reduce_fusion.12
  7.9 0.1 compare_reduce_fusion.13
  8.0 0.1 compare_reduce_fusion.14
  8.2 0.1 compare_reduce_fusion.15
  8.3 0.1 compare_reduce_fusion.16
  8.4 0.1 compare_reduce_fusion.17
  8.5 0.1 compare_reduce_fusion.18
  8.8 0.1 compare_reduce_fusion.2
  8.9 0.1 compare_reduce_fusion.20
  9.0 0.1 compare_reduce_fusion.21
  9.1 0.1 compare_reduce_fusion.22
  10.4 1.8 fusion.106
  12.2 2.1 fusion.105
  14.3 4.6 compare_select_fusion.4
  18.9 15.4 %compare_and_fusion.2 = (pred[2048]{0:T(1024)(128)(4,1)S(1)}, s32[2048]{0:T(1024)S(1)}) fusion(pred[2048]{0:T(1024)(128)(4,1)S(1)} %compare_reduce_fusion, pred[2048]{0:T(1024)(128)(4,1)S(1)} %compare_reduce_fusion.1, pred[2048]{0:T(1024)(128)(4,1)S(1)} %compare_reduce_fusion.2, pred[2048]{0:T(1024)(128)(4,1)S(1)} %compare_reduce_fusion.3, ...), kind=kLoop, calls=%fused_computation.236 | loop fusion | flops 165888 | bytes 69732 | tf_op jit(solution)/shard_map/jit(_take)/and | solution.py:43
  34.4 43.7 %all-gather.7.cloned.1.call-done = bf16[2048,2048]{1,0:T(8,128)(2,1)} async-done(((bf16[64,2048]{1,0:T(8,128)(2,1)}), bf16[2048,2048]{1,0:T(8,128)(2,1)}) %all-gather.7.cloned.1.call-update) | async-done | bytes 8388624 | tf_op jit(solution)/shard_map/all_gather | solution.py:39
  78.0 20.8 %gather_fusion = bf16[2048,2048]{1,0:T(8,128)(2,1)} fusion(bf16[2048,2048]{1,0:T(8,128)(2,1)} %all-gather.7.cloned.1.call-done, s32[2048]{0:T(1024)S(1)} %broadcast_clamp_fusion.1), kind=kCustom, calls=%fused_computation | custom fusion | bytes 16785408 | tf_op jit(solution)/shard_map/jit(_take)/gather | solution.py:43
  98.8 5.7 %fusion.36 = f32[2048]{0:T(1024)S(1)} fusion(bf16[2048,2048]{1,0:T(8,128)(2,1)} %gather_fusion, pred[2048]{0:T(1024)(128)(4,1)S(1)} %get-tuple-element.73), kind=kLoop, calls=%fused_computation.36 | loop fusion | flops 16775168 | bytes 8398848 | tf_op jit(solution)/shard_map/reduce_sum | solution.py:46
  104.6 10.7 %psum.7 = f32[2048]{0:T(1024)S(1)} all-reduce(f32[2048]{0:T(1024)S(1)} %fusion.36), channel_id=1, replica_groups=mesh['section'=2,'cp'=16,'tp'=4] {'tp'}, use_global_device_ids=true, to_apply=%region_5.6 | all-reduce | flops 2048 | bytes 16384 | tf_op jit(solution)/shard_map/psum | solution.py:47
  115.3 20.0 %fusion.38 = f32[2048,3,512]{2,0,1:T(8,128)} fusion(f32[2048]{0:T(1024)S(1)} %add_rsqrt_fusion, f32[2048]{0:T(1024)S(1)} %bitcast.118, bf16[1,3,2048,512]{3,2,1,0:T(8,128)(2,1)} %param.14, bf16[2048,2048]{1,0:T(8,128)(2,1)} %gather_fusion, pred[2048]{0:T(1024)(128)(4,1)S(1)} %get-tuple-element.73), kind=kOutput, calls=%fused_computation.38 | convolution fusion | flops 12905873408 | bytes 27281408 | tf_op jit(solution)/shard_map/rd,kdc->rkc/dot_general | solution.py:66
  135.4 111.7 %reduce-scatter.3.cloned.1.call-done = f32[512,3,512]{2,0,1:T(8,128)} async-done(((f32[2048,3,512]{2,0,1:T(8,128)}), f32[512,3,512]{2,0,1:T(8,128)}) %reduce-scatter.3.cloned.1.call-update) | async-done | bytes 3145744 | tf_op jit(solution)/shard_map/reduce_scatter | solution.py:65
  247.2 2.1 convert_element_type.41
  249.3 1.1 copy-done.1
  250.4 1.0 fusion.100
  251.5 0.5 all-gather.13.cloned.1.call-update
  252.1 0.2 all-gather.9.cloned.1.call-start
  252.3 0.2 reduce-window.8
  252.8 1.7 fusion.98
  255.7 26.5 %all-gather.11.cloned.1.call-done = bf16[2048,1,512]{2,0,1:T(8,128)(2,1)} async-done(((bf16[512,1,512]{2,0,1:T(8,128)(2,1)}), bf16[2048,1,512]{2,0,1:T(8,128)(2,1)}) %all-gather.11.cloned.1.call-update) | async-done | bytes 2097168 | tf_op jit(solution)/shard_map/all_gather | solution.py:72
  282.2 4.0 reshape.639
  286.2 28.4 %all-gather.13.cloned.1.call-done = bf16[2048,1,512]{2,0,1:T(8,128)(2,1)} async-done(((bf16[512,1,512]{2,0,1:T(8,128)(2,1)}), bf16[2048,1,512]{2,0,1:T(8,128)(2,1)}) %all-gather.13.cloned.1.call-update) | async-done | bytes 2097168 | tf_op jit(solution)/shard_map/all_gather | solution.py:73
  314.6 4.0 reshape.640
  318.6 13.3 %conditional.2 = (f32[1,4,256]{2,1,0:T(4,128)S(1)}, f32[1,4,256,128]{3,2,1,0:T(8,128)}) conditional(s32[]{:T(128)} %convert_element_type.38, () %tuple.29, (pred[256,2048]{1,0:T(8,128)(4,1)S(1)}, bf16[512,3,512]{2,0,1:T(8,128)(2,1)}, bf16[2048,4,128]{2,1,0:T(4,128)(2,1)}, bf16[2048,4,128]{2,1,0:T(4,128)(2,1)}) %tuple.128), branch_computations={%region_7.8_spmd, %region_8.11_spmd} | conditional | flops 1101003776 | bytes 43802668 | solution.py:106
  318.6 2.6 copy.25
  321.2 1.1 slice.111
  322.3 3.7 fusion
  326.0 3.4 fusion.9
  329.4 2.5 fusion.2
  331.9 12.8 %conditional.3 = (f32[1,4,256]{2,1,0:T(4,128)S(1)}, f32[1,4,256,128]{3,2,1,0:T(8,128)S(1)}) conditional(s32[]{:T(128)} %convert_element_type.42, () %tuple.31, (pred[256,2048]{1,0:T(8,128)(4,1)S(1)}, bf16[512,3,512]{2,0,1:T(8,128)(2,1)}, bf16[2048,4,128]{2,1,0:T(4,128)(2,1)}, bf16[2048,4,128]{2,1,0:T(4,128)(2,1)}) %tuple.129), branch_computations={%region_12.13_spmd, %region_13.16_spmd} | conditional | flops 1101003776 | bytes 43802668 | solution.py:106
  332.2 2.6 copy.28
  334.8 1.1 slice.112
  335.9 3.7 fusion.17
  339.6 2.6 fusion.26
  342.2 2.5 fusion.19
  344.7 1.4 fusion.48
  346.1 0.4 copy.31
  346.6 0.9 copy.52
  349.8 0.4 compare_reduce_fusion.49
  350.2 0.7 fusion.104
  350.9 0.7 fusion.103
  351.7 4.6 compare_select_fusion.10
  356.3 15.4 %compare_and_fusion.3 = (pred[2048]{0:T(1024)(128)(4,1)S(1)}, s32[2048]{0:T(1024)S(1)}) fusion(pred[2048]{0:T(1024)(128)(4,1)S(1)} %compare_reduce_fusion.25, pred[2048]{0:T(1024)(128)(4,1)S(1)} %compare_reduce_fusion.26, pred[2048]{0:T(1024)(128)(4,1)S(1)} %compare_reduce_fusion.27, pred[2048]{0:T(1024)(128)(4,1)S(1)} %compare_reduce_fusion.28, ...), kind=kLoop, calls=%fused_computation.237 | loop fusion | flops 165888 | bytes 69732 | tf_op jit(solution)/shard_map/jit(_take)/and | solution.py:132
  371.7 0.1 compare_select_fusion
  371.9 6.6 %all-gather.9.cloned.1.call-done = bf16[2048,512]{1,0:T(8,128)(2,1)} async-done(((bf16[512,512]{1,0:T(8,128)(2,1)}), bf16[2048,512]{1,0:T(8,128)(2,1)}) %all-gather.9.cloned.1.call-update) | async-done | bytes 2097168 | tf_op jit(solution)/shard_map/all_gather | solution.py:120
  378.5 11.1 %gather_fusion.1 = bf16[2048,512]{1,0:T(8,128)(2,1)} fusion(bf16[2048,512]{1,0:T(8,128)(2,1)} %all-gather.9.cloned.1.call-done, s32[2048]{0:T(1024)S(1)} %broadcast_clamp_fusion), kind=kCustom, calls=%fused_computation.1 | custom fusion | bytes 4202496 | tf_op jit(solution)/shard_map/jit(_take)/gather | solution.py:132
  389.5 8.5 %convolution_convert_fusion = bf16[2048,2048]{1,0:T(8,128)(2,1)} fusion(bf16[1,512,2048]{2,1,0:T(8,128)(2,1)S(1)} %copy-done, bf16[2048,512]{1,0:T(8,128)(2,1)} %gather_fusion.1, pred[2048]{0:T(1024)(128)(4,1)S(1)} %get-tuple-element.69), kind=kOutput, calls=%fused_computation.42 | convolution fusion | flops 4300210176 | bytes 12584960 | tf_op jit(solution)/shard_map/dot_general | solution.py:135
  398.0 102.8 %reduce-scatter.5.cloned.1.call-done = bf16[128,2048]{1,0:T(8,128)(2,1)} async-done(((bf16[2048,2048]{1,0:T(8,128)(2,1)}), bf16[128,2048]{1,0:T(8,128)(2,1)}) %reduce-scatter.5.cloned.1.call-update) | async-done | bytes 524304 | tf_op jit(solution)/shard_map/reduce_scatter | solution.py:134
  500.8 10.7 %all_to_all.5 = bf16[2,64,2048]{2,1,0:T(8,128)(2,1)S(1)} all-to-all(bf16[2,64,2048]{2,1,0:T(8,128)(2,1)} %bitcast.108), channel_id=1, replica_groups=mesh['section'=2,'cp'=16,'tp'=4] {'section'}, dimensions={0} | all-to-all | bytes 1048576 | tf_op jit(solution)/shard_map/all_to_all | solution.py:141
  511.6 0.8 copy.62
  (69 shorter events, 4.2 us)
Async XLA Ops:
  6.5 383.0 %copy-start = (bf16[1,512,2048]{2,1,0:T(8,128)(2,1)S(1)}, bf16[1,512,2048]{2,1,0:T(8,128)(2,1)}, u32[]{:S(2)}) copy-start(bf16[1,512,2048]{2,1,0:T(8,128)(2,1)} %param.15) | copy-start | bytes 6291460
  6.5 71.5 %all-gather.7.cloned.1.call-start = ((), (), s32[]{:S(2)}) async-start(), calls=%async_computation.3 | async-start | bytes 8650752 | tf_op jit(solution)/shard_map/all_gather | solution.py:39
  7.3 239.9 %reduce-scatter.3.cloned.1.call-start = ((), (), s32[]{:S(2)}) async-start(), calls=%async_computation.4 | async-start | bytes 15728640 | tf_op jit(solution)/shard_map/reduce_scatter | solution.py:65
  98.8 16.5 %copy-start.5 = (f32[1,2048]{1,0:T(1,128)S(1)}, f32[1,2048]{1,0:T(1,128)}, u32[]{:S(2)}) copy-start(f32[1,2048]{1,0:T(1,128)} %param.13) | copy-start | bytes 24580
  135.4 116.9 %copy-start.6 = (s32[2]{0:T(128)S(1)}, s32[2]{0:T(128)}, u32[]{:S(2)}) copy-start(s32[2]{0:T(128)} %param.11) | copy-start | bytes 28
  135.4 146.8 %all-gather.11.cloned.1.call-start = ((), (), s32[]{:S(2)}) async-start(), calls=%async_computation.7 | async-start | bytes 2621440 | tf_op jit(solution)/shard_map/all_gather | solution.py:72
  249.3 1.1 copy-start.1
  251.5 63.1 %all-gather.13.cloned.1.call-start = ((), (), s32[]{:S(2)}) async-start(), calls=%async_computation.8 | async-start | bytes 2621440 | tf_op jit(solution)/shard_map/all_gather | solution.py:73
  252.1 126.4 %all-gather.9.cloned.1.call-start = ((), (), s32[]{:S(2)}) async-start(), calls=%async_computation.5 | async-start | bytes 2621440 | tf_op jit(solution)/shard_map/all_gather | solution.py:120
  321.1 4.8 copy-start.2
  331.9 18.2 %copy-start.4 = (s32[32]{0:T(128)S(1)}, s32[32]{0:T(128)}, u32[]{:S(2)}) copy-start(s32[32]{0:T(128)} %param.12) | copy-start | bytes 388
  334.8 4.8 copy-start.3
  347.5 153.4 %reduce-scatter.5.cloned.1.call-start = ((), (), s32[]{:S(2)}) async-start(), calls=%async_computation.6 | async-start | bytes 8912896 | tf_op jit(solution)/shard_map/reduce_scatter | solution.py:134
Sparse Core Ops, SparseCore 0:
  9.1 68.9 all-gather.6
  135.5 111.6 reduce-scatter.2
  251.6 30.5 all-gather.10
  283.7 30.8 all-gather.12
  347.6 30.8 all-gather.8
  398.1 102.6 reduce-scatter.4
where the time goes:
time: 521 us; the launch traced here: 519 us
  waiting for transfers between devices  321 us (62%)
  other arithmetic  62.2 us (12%)
  local copies, waits for them, and re-layouts  57 us (11%)
  matrix products  42 us (8%)
  blocking collectives  21.5 us (4%)
  between operations  14.9 us (3%)
    reduce_scatter x1, waiting for transfers between devices, on_device(): lax.psum_scatter(jnp.einsum('rd,kdc->rkc', normed, qkv_weights, preferred...  112 us
    reduce_scatter x1, waiting for transfers between devices, on_device(): lax.psum_scatter(jnp.dot(ordered, out_weight, preferred_element_type=jnp....  103 us
    all_gather x1, waiting for transfers between devices, on_device(): lax.all_gather(rollout_rows, ('section', 'cp'), axis=0, tiled=True)  43.7 us
    all_gather x1, waiting for transfers between devices, on_device(): value_part = lax.all_gather(projected[:, 2], 'tp', axis=0, tiled=True)  28.4 us
    all_gather x1, waiting for transfers between devices, on_device(): key_part = lax.all_gather(projected[:, 1], 'tp', axis=0, tiled=True)  26.5 us
    gather x1, local copies, waits for them, and re-layouts, on_device(): rows_in = jnp.take(actor_rows, source, axis=0)  20.8 us
    dot_general x1, matrix products, on_device(): jnp.einsum('rd,kdc->rkc', normed, qkv_weights, preferred_element_type=jnp...  20 us
    and x1, other arithmetic, on_device(): jnp.take(gathered, layout_row(packed_pos, tokens, tp_count), axis=0)  15.4 us
  transfers between devices with their start and end apart: 6, of which 6 were waited for; matrix products, arithmetic and copies ran while one was open for 11% of the time, Pallas kernels for 0%

commit v1 on v0

v1 whole, which is shorter than its diff:
```python
import math

import jax
import jax.numpy as jnp
from jax import lax
from jax.sharding import PartitionSpec as P

D = 8192
HEAD = 128


def on_device(rollout_rows, lengths, block_owner, norm_gain, w_qkv, w_out):
    tp_count = lax.axis_size("tp")
    cp_count = lax.axis_size("cp")
    sections = lax.axis_size("section")
    own_rows, width_here = rollout_rows.shape
    blocks = sections * cp_count
    tokens = own_rows * blocks

    rows_in = lax.all_gather(rollout_rows, ("cp", "section"), axis=0, tiled=True)
    layout_rows = jnp.arange(tokens, dtype=jnp.int32)
    cp_of = layout_rows // (sections * own_rows)
    section_of = layout_rows // own_rows % sections
    actor_block = section_of * cp_count + cp_of
    block_ids = jnp.arange(blocks, dtype=jnp.int32)
    packed_block = jnp.sum(
        jnp.where(block_owner[None, :] == block_ids[:, None], block_ids[None, :], 0), axis=1
    )
    position = packed_block[actor_block] * own_rows + layout_rows % own_rows
    seq_ends = jnp.cumsum(lengths)
    sequence = jnp.sum((position[:, None] >= seq_ends[None, :]).astype(jnp.int32), axis=1)

    rows_f32 = rows_in.astype(jnp.float32)
    squares = jnp.sum(jnp.square(rows_f32), axis=1)
    total_squares = lax.psum(squares, "tp")
    inverse_rms = lax.rsqrt(total_squares / D + 1e-05)
    scaled = (rows_f32 * norm_gain[0][None, :]).astype(jnp.bfloat16)

    qkv_weights = w_qkv[0]
    group_cols = qkv_weights.shape[2]
    heads_here = group_cols // HEAD
    weights4 = qkv_weights.reshape(3, width_here, heads_here, HEAD)
    partial = jnp.einsum(
        "rd,kdje->jrke", scaled, weights4, preferred_element_type=jnp.float32
    ).astype(jnp.bfloat16)
    partial = partial.reshape(heads_here * tokens, 3 * HEAD)
    one_head = lax.psum_scatter(partial, "tp", scatter_dimension=0, tiled=True)
    one_head = one_head.reshape(tokens, 3, HEAD)
    one_head = (one_head.astype(jnp.float32) * inverse_rms[:, None, None]).astype(jnp.bfloat16)
    queries = one_head[:, 0]
    key_rows = one_head[:, 1]
    value_rows = one_head[:, 2]

    allowed = (sequence[:, None] == sequence[None, :]) & (position[None, :] <= position[:, None])
    scores = jnp.dot(queries, key_rows.T, preferred_element_type=jnp.float32) / math.sqrt(HEAD)
    scores = jnp.where(allowed, scores, -1e30)
    row_peak = jnp.max(scores, axis=1, keepdims=True)
    weights = jnp.where(allowed, jnp.exp(scores - row_peak), 0.0)
    row_total = jnp.sum(weights, axis=1, keepdims=True)
    probabilities = weights.astype(jnp.bfloat16)
    mixed = jnp.dot(probabilities, value_rows, preferred_element_type=jnp.float32)
    attended = (mixed / row_total).astype(jnp.bfloat16)

    group_att = lax.all_gather(attended, "tp", axis=0, tiled=False)
    out_weight = w_out[0].reshape(tp_count, HEAD, width_here)
    partial_out = jnp.einsum(
        "jre,jew->rw", group_att, out_weight, preferred_element_type=jnp.float32
    ).astype(jnp.bfloat16)
    summed = lax.psum_scatter(partial_out, "cp", scatter_dimension=0, tiled=True)
    branch = summed.reshape(sections, own_rows, width_here)
    return lax.all_to_all(branch, "section", split_axis=0, concat_axis=0, tiled=True)


def solution(mesh):
    return jax.shard_map(
        on_device,
        mesh=mesh,
        in_specs=(
            P(("section", "cp"), "tp"),
            P(),
            P(),
            P("section", "tp"),
            P("section", None, "tp", "cp"),
            P("section", "cp", "tp"),
        ),
        out_specs=P(None, ("section", "cp"), "tp"),
        check_vma=False,
    )
```

time: 521 us -> 394 us (0.76)
  waiting for transfers between devices: 321 us -> 245 us
  other arithmetic: 62.2 us -> 37.1 us
  local copies, waits for them, and re-layouts: 57 us -> 36 us
    reduce_scatter x2, waiting for transfers between devices: 215 us -> 128 us  [the longest x1 103 us: on_device(): lax.psum_scatter(partial_out, 'cp', scatter_dimension=0, tiled=True)]
    gather x6 -> x2, local copies, waits for them, and re-layouts: 37.2 us -> 1.44 us  [on_device(): position = packed_block[actor_block] * own_rows + layout_rows % own_rows]
    and x2 -> x0, other arithmetic: 30.8 us -> none  [the longest x1 15.4 us: on_device(): jnp.take(gathered, layout_row(packed_pos, tokens, tp_count), axis=0)]
    add x1, other arithmetic: 0.01 us -> 15.8 us  [on_device(): position = packed_block[actor_block] * own_rows + layout_rows % own_rows]
    all_gather x4 -> x2, waiting for transfers between devices: 105 us -> 117 us  [the longest x1 86.4 us: on_device(): lax.all_gather(rollout_rows, ('cp', 'section'), axis=0, tiled=True)]
    convert_element_type x1, local copies, waits for them, and re-layouts: 0.41 us -> 11.3 us  [on_device(): partial = jnp.einsum('rd,kdje->jrke', scaled, weights4, preferred_element...]
    unnamed x12 -> x10, local copies, waits for them, and re-layouts: 2.82 us -> 13.6 us
    gather x54 -> x26, other arithmetic: 14.9 us -> 6.27 us  [on_device(): position = packed_block[actor_block] * own_rows + layout_rows % own_rows]
  transfers between devices with their start and end apart: 6 -> 4, of which waited for: 6 -> 4; matrix products, arithmetic and copies ran while one was open for 11% -> 10% of each run, Pallas kernels for 0% -> 0%
where the time goes in v1:
time: 394 us; the launch traced here: 393 us
  waiting for transfers between devices  245 us (62%)
  matrix products  38.1 us (10%)
  other arithmetic  37.1 us (9%)
  local copies, waits for them, and re-layouts  36 us (9%)
  blocking collectives  22.9 us (6%)
  between operations  13.2 us (3%)
    reduce_scatter x1, waiting for transfers between devices, on_device(): lax.psum_scatter(partial_out, 'cp', scatter_dimension=0, tiled=True)  103 us
    all_gather x1, waiting for transfers between devices, on_device(): lax.all_gather(rollout_rows, ('cp', 'section'), axis=0, tiled=True)  86.4 us
    all_gather x1, waiting for transfers between devices, on_device(): group_att = lax.all_gather(attended, 'tp', axis=0, tiled=False)  30.5 us
    reduce_scatter x1, waiting for transfers between devices, on_device(): one_head = lax.psum_scatter(partial, 'tp', scatter_dimension=0, tiled=True)  25 us
    dot_general x1, matrix products, on_device(): jnp.einsum('rd,kdje->jrke', scaled, weights4, preferred_element_type=jnp....  18.6 us
    add x1, other arithmetic, on_device(): position = packed_block[actor_block] * own_rows + layout_rows % own_rows  15.8 us
    unnamed x10, local copies, waits for them, and re-layouts  13.6 us
    psum x1, blocking collectives, on_device(): total_squares = lax.psum(squares, 'tp')  12.1 us
  transfers between devices with their start and end apart: 4, of which 4 were waited for; matrix products, arithmetic and copies ran while one was open for 10% of the time, Pallas kernels for 0%

profile of v1, /device:TPU:0, one launch (start us, length us, event | category | flops | bytes accessed | tf_op | source)
XLA Modules:
  0.0 392.9 jit_solution(9491372023478342441)
XLA Ops:
  6.5 0.0 copy-start
  6.5 0.0 copy-start.1
  6.5 0.0 all-gather.4.cloned.1.call-start
  6.5 0.7 all-gather.4.cloned.1.call-update
  7.3 0.0 reduce-scatter.3.cloned.1.call-start
  7.3 9.7 %reshape_squeeze.6 = bf16[3,2048,4,128]{3,2,1,0:T(4,128)(2,1)} reshape(bf16[1,3,2048,512]{3,2,1,0:T(8,128)(2,1)} %param.10) | data formatting | bytes 12582912 | tf_op jit(solution)/shard_map/reshape;squeeze | solution.py:42
  17.0 86.4 %all-gather.4.cloned.1.call-done = bf16[2048,2048]{1,0:T(8,128)(2,1)} async-done(((bf16[64,2048]{1,0:T(8,128)(2,1)}), bf16[2048,2048]{1,0:T(8,128)(2,1)}) %all-gather.4.cloned.1.call-update) | async-done | bytes 8388624 | tf_op jit(solution)/shard_map/all_gather | solution.py:20
  103.4 0.0 copy-done.1
  103.4 18.6 %convert_bitcast_fusion = bf16[4,2048,3,128]{3,1,0,2:T(8,128)(2,1)} fusion(bf16[3,2048,4,128]{3,2,1,0:T(4,128)(2,1)} %reshape_squeeze.6, bf16[2048,2048]{1,0:T(8,128)(2,1)} %all-gather.4.cloned.1.call-done, f32[2048]{0:T(1024)S(1)} %bitcast.85), kind=kOutput, calls=%fused_computation.16 | convolution fusion | flops 12900630528 | bytes 20979712 | tf_op jit(solution)/shard_map/rd,kdje->jrke/dot_general | solution.py:43
  122.0 11.3 %copy.14 = bf16[4,2048,3,128]{1,0,3,2:T(4,128)(2,1)} copy(bf16[4,2048,3,128]{3,1,0,2:T(8,128)(2,1)} %convert_bitcast_fusion) | data formatting | bytes 12582912 | tf_op jit(solution)/shard_map/convert_element_type | solution.py:45
  133.2 0.0 copy-start.2
  133.2 12.7 %copy.19 = bf16[48,8,4,2048]{3,1,2,0:T(8,128)(2,1)} copy(bf16[48,8,4,2048]{3,2,1,0:T(4,128)(2,1)} %bitcast.79) | data formatting | bytes 12582912
  146.0 0.0 reduce-scatter.3.cloned.1.call-update
  146.0 0.2 all-gather.6.cloned.1.call-start
  146.2 0.0 copy-done.2
  146.3 0.2 reduce-window.8
  146.4 0.1 compare_reduce_fusion
  146.5 0.1 compare_reduce_fusion.1
  146.6 0.1 compare_reduce_fusion.10
  146.6 0.1 compare_reduce_fusion.11
  146.7 0.1 compare_reduce_fusion.12
  146.8 0.1 compare_reduce_fusion.13
  146.9 0.1 compare_reduce_fusion.14
  146.9 0.1 compare_reduce_fusion.15
  147.0 0.1 compare_reduce_fusion.16
  147.1 0.1 compare_reduce_fusion.17
  147.2 0.1 compare_reduce_fusion.18
  147.3 0.1 compare_reduce_fusion.19
  147.3 0.1 compare_reduce_fusion.2
  147.4 0.1 compare_reduce_fusion.20
  147.5 0.1 compare_reduce_fusion.21
  147.6 0.1 compare_reduce_fusion.22
  147.6 0.1 compare_reduce_fusion.23
  147.7 0.1 compare_reduce_fusion.24
  147.8 0.1 compare_reduce_fusion.3
  147.9 0.1 compare_reduce_fusion.4
  147.9 0.1 compare_reduce_fusion.5
  148.0 0.1 compare_reduce_fusion.6
  148.1 0.1 compare_reduce_fusion.7
  148.2 0.1 compare_reduce_fusion.8
  148.2 0.1 compare_reduce_fusion.9
  148.3 0.0 copy-done.3
  148.3 0.1 select_reduce_fusion
  148.4 0.7 fusion.36
  149.1 0.7 fusion.35
  149.9 4.4 %compare_select_fusion.3 = s32[2048,1]{0,1:T(1,128)S(1)} fusion(s32[]{:T(128)} %bitcast.25, s32[]{:T(128)} %bitcast.26, s32[]{:T(128)} %bitcast.27, s32[]{:T(128)} %bitcast.28, s32[]{:T(128)} %bitcast.29, s32[]{:T(128)} %bitcast.31, s32[]{:T(128)} %bitcast.30), kind=kLoop, calls=%fused_computation.53 | loop fusion | flops 86016 | bytes 8220 | tf_op jit(solution)/shard_map/gather | solution.py:29
  154.3 15.8 %fusion.25 = s32[2048]{0:T(1024)S(1)} fusion(pred[2048]{0:T(1024)(128)(4,1)S(1)} %compare_reduce_fusion, pred[2048]{0:T(1024)(128)(4,1)S(1)} %compare_reduce_fusion.1, pred[2048]{0:T(1024)(128)(4,1)S(1)} %compare_reduce_fusion.2, pred[2048]{0:T(1024)(128)(4,1)S(1)} %compare_reduce_fusion.3, pred[2048]{0:T(1024)(128)(4,1)S(1)} %compare_reduce_fusion.4, ...), kind=kLoop, calls=%fused_computation.72 | loop fusion | flops 67584 | bytes 67684 | tf_op jit(solution)/shard_map/add | solution.py:29
  170.1 0.1 fusion.24
  170.2 5.1 %fusion.1 = f32[2048]{0:T(1024)S(1)} fusion(bf16[2048,2048]{1,0:T(8,128)(2,1)} %all-gather.4.cloned.1.call-done), kind=kLoop, calls=%fused_computation.3 | loop fusion | flops 12580864 | bytes 8396800 | tf_op jit(solution)/shard_map/reduce_sum | solution.py:34
  175.2 12.1 %psum.7 = f32[2048]{0:T(1024)S(1)} all-reduce(f32[2048]{0:T(1024)S(1)} %fusion.1), channel_id=1, replica_groups=mesh['section'=2,'cp'=16,'tp'=4] {'tp'}, use_global_device_ids=true, to_apply=%region_5.6 | all-reduce | flops 2048 | bytes 16384 | tf_op jit(solution)/shard_map/psum | solution.py:35
  187.4 25.0 %reduce-scatter.3.cloned.1.call-done = bf16[2048,384]{0,1:T(8,128)(2,1)} async-done(((bf16[8192,384]{0,1:T(8,128)(2,1)}), bf16[2048,384]{0,1:T(8,128)(2,1)}) %reduce-scatter.3.cloned.1.call-update) | async-done | bytes 1572880 | tf_op jit(solution)/shard_map/reduce_scatter | solution.py:47
  212.4 1.9 fusion.16
  214.2 4.4 %fusion.2 = (f32[2048]{0:T(1024)S(1)}, f32[2048,2048]{0,1:T(8,128)S(1)}) fusion(s32[2048]{0:T(1024)S(1)} %fusion.25, s32[2048]{0:T(1024)S(1)} %fusion.24, bf16[2048,3,128]{0,2,1:T(8,128)(2,1)S(1)} %fusion.16), kind=kOutput, calls=%fused_computation.8 | convolution fusion | flops 1098905600 | bytes 17866752 | tf_op jit(solution)/shard_map/dot_general | solution.py:55
  218.7 7.7 %fusion.3 = f32[2048]{0:T(1024)S(1)} fusion(f32[2048,2048]{0,1:T(8,128)S(1)} %get-tuple-element.38, f32[2048]{0:T(1024)S(1)} %get-tuple-element.37, s32[2048]{0:T(1024)S(1)} %fusion.25, s32[2048]{0:T(1024)S(1)} %fusion.24), kind=kLoop, calls=%fused_computation.9 | loop fusion | flops 33552384 | bytes 16809984 | tf_op jit(solution)/shard_map/reduce_sum | solution.py:59
  226.3 6.7 %fusion.20 = bf16[2048,128]{1,0:T(8,128)(2,1)} fusion(f32[2048,2048]{0,1:T(8,128)S(1)} %get-tuple-element.38, f32[2048]{0:T(1024)S(1)} %get-tuple-element.37, s32[2048]{0:T(1024)S(1)} %fusion.25, s32[2048]{0:T(1024)S(1)} %fusion.24, bf16[2048,3,128]{0,2,1:T(8,128)(2,1)S(1)} %fusion.16, f32[2048]{0:T(1024)S(1)} %fusion.3), kind=kOutput, calls=%fused_computation.20 | convolution fusion | flops 1107820544 | bytes 17874944 | tf_op jit(solution)/shard_map/dot_general | solution.py:61
  233.1 0.0 all-gather.6.cloned.1.call-update
  233.1 0.0 reduce-scatter.5.cloned.1.call-start
  233.1 30.5 %all-gather.6.cloned.1.call-done = bf16[8192,128]{1,0:T(8,128)(2,1)} async-done(((bf16[2048,128]{1,0:T(8,128)(2,1)}), bf16[8192,128]{1,0:T(8,128)(2,1)}) %all-gather.6.cloned.1.call-update) | async-done | bytes 2097168 | tf_op jit(solution)/shard_map/all_gather | solution.py:64
  263.6 0.0 copy-done
  263.6 8.4 %bitcast_convert_fusion = bf16[2048,2048]{1,0:T(8,128)(2,1)} fusion(bf16[4,2048,128]{2,1,0:T(8,128)(2,1)} %bitcast.84, bf16[4,128,2048]{2,1,0:T(8,128)(2,1)S(1)} %bitcast.77), kind=kOutput, calls=%fused_computation.4 | convolution fusion | flops 4299161600 | bytes 12582912 | tf_op jit(solution)/shard_map/jre,jew->rw/dot_general | solution.py:66
  272.0 0.0 reduce-scatter.5.cloned.1.call-update
  272.0 102.8 %reduce-scatter.5.cloned.1.call-done = bf16[128,2048]{1,0:T(8,128)(2,1)} async-done(((bf16[2048,2048]{1,0:T(8,128)(2,1)}), bf16[128,2048]{1,0:T(8,128)(2,1)}) %reduce-scatter.5.cloned.1.call-update) | async-done | bytes 524304 | tf_op jit(solution)/shard_map/reduce_scatter | solution.py:69
  374.8 10.8 %all_to_all.5 = bf16[2,64,2048]{2,1,0:T(8,128)(2,1)S(1)} all-to-all(bf16[2,64,2048]{2,1,0:T(8,128)(2,1)} %bitcast.81), channel_id=1, replica_groups=mesh['section'=2,'cp'=16,'tp'=4] {'section'}, dimensions={0} | all-to-all | bytes 1048576 | tf_op jit(solution)/shard_map/all_to_all | solution.py:71
  385.6 0.8 copy.25
  (2 shorter events, 0.0 us)
Async XLA Ops:
  6.5 257.1 %copy-start = (bf16[1,512,2048]{2,1,0:T(8,128)(2,1)S(1)}, bf16[1,512,2048]{2,1,0:T(8,128)(2,1)}, u32[]{:S(2)}) copy-start(bf16[1,512,2048]{2,1,0:T(8,128)(2,1)} %param.11) | copy-start | bytes 6291460
  6.5 96.9 %copy-start.1 = (f32[1,2048]{1,0:T(1,128)S(1)}, f32[1,2048]{1,0:T(1,128)}, u32[]{:S(2)}) copy-start(f32[1,2048]{1,0:T(1,128)} %param.9) | copy-start | bytes 24580
  6.5 96.9 %all-gather.4.cloned.1.call-start = ((), (), s32[]{:S(2)}) async-start(), calls=%async_computation.3 | async-start | bytes 8650752 | tf_op jit(solution)/shard_map/all_gather | solution.py:20
  7.3 205.1 %reduce-scatter.3.cloned.1.call-start = ((), (), s32[]{:S(2)}) async-start(), calls=%async_computation.4 | async-start | bytes 7864320 | tf_op jit(solution)/shard_map/reduce_scatter | solution.py:47
  133.2 13.0 %copy-start.2 = (s32[2]{0:T(128)S(1)}, s32[2]{0:T(128)}, u32[]{:S(2)}) copy-start(s32[2]{0:T(128)} %param.7) | copy-start | bytes 28
  133.2 15.1 %copy-start.3 = (s32[32]{0:T(128)S(1)}, s32[32]{0:T(128)}, u32[]{:S(2)}) copy-start(s32[32]{0:T(128)} %param.8) | copy-start | bytes 388
  146.0 117.6 %all-gather.6.cloned.1.call-start = ((), (), s32[]{:S(2)}) async-start(), calls=%async_computation.6 | async-start | bytes 2621440 | tf_op jit(solution)/shard_map/all_gather | solution.py:64
  233.1 141.7 %reduce-scatter.5.cloned.1.call-start = ((), (), s32[]{:S(2)}) async-start(), calls=%async_computation.5 | async-start | bytes 8912896 | tf_op jit(solution)/shard_map/reduce_scatter | solution.py:69
Sparse Core Ops, SparseCore 0:
  9.0 94.3 all-gather.3
  146.1 66.1 reduce-scatter.2
  233.2 30.3 all-gather.5
  272.1 102.6 reduce-scatter.4

commit v2 on v1

--- a/solution.py
+++ b/solution.py
@@ -17,18 +17,22 @@
     blocks = sections * cp_count
     tokens = own_rows * blocks
 
-    rows_in = lax.all_gather(rollout_rows, ("cp", "section"), axis=0, tiled=True)
-    layout_rows = jnp.arange(tokens, dtype=jnp.int32)
-    cp_of = layout_rows // (sections * own_rows)
-    section_of = layout_rows // own_rows % sections
-    actor_block = section_of * cp_count + cp_of
+    rows_in = lax.all_gather(rollout_rows, ("section", "cp"), axis=0, tiled=True)
     block_ids = jnp.arange(blocks, dtype=jnp.int32)
     packed_block = jnp.sum(
         jnp.where(block_owner[None, :] == block_ids[:, None], block_ids[None, :], 0), axis=1
     )
-    position = packed_block[actor_block] * own_rows + layout_rows % own_rows
+    inner = jnp.arange(own_rows, dtype=jnp.int32)
+    position = (packed_block[:, None] * own_rows + inner[None, :]).reshape(tokens)
+    query_position = (
+        packed_block.reshape(sections, cp_count).T.reshape(blocks)[:, None] * own_rows
+        + inner[None, :]
+    ).reshape(tokens)
     seq_ends = jnp.cumsum(lengths)
     sequence = jnp.sum((position[:, None] >= seq_ends[None, :]).astype(jnp.int32), axis=1)
+    query_sequence = jnp.sum(
+        (query_position[:, None] >= seq_ends[None, :]).astype(jnp.int32), axis=1
+    )
 
     rows_f32 = rows_in.astype(jnp.float32)
     squares = jnp.sum(jnp.square(rows_f32), axis=1)
@@ -39,19 +43,33 @@
     qkv_weights = w_qkv[0]
     group_cols = qkv_weights.shape[2]
     heads_here = group_cols // HEAD
-    weights4 = qkv_weights.reshape(3, width_here, heads_here, HEAD)
-    partial = jnp.einsum(
-        "rd,kdje->jrke", scaled, weights4, preferred_element_type=jnp.float32
-    ).astype(jnp.bfloat16)
-    partial = partial.reshape(heads_here * tokens, 3 * HEAD)
+    partial = jnp.stack(
+        [
+            jnp.einsum(
+                "rd,kde->kre",
+                scaled,
+                qkv_weights[:, :, j * HEAD : (j + 1) * HEAD],
+                preferred_element_type=jnp.float32,
+            ).astype(jnp.bfloat16)
+            for j in range(heads_here)
+        ]
+    )
+    partial = partial.reshape(heads_here * 3 * tokens, HEAD)
     one_head = lax.psum_scatter(partial, "tp", scatter_dimension=0, tiled=True)
-    one_head = one_head.reshape(tokens, 3, HEAD)
-    one_head = (one_head.astype(jnp.float32) * inverse_rms[:, None, None]).astype(jnp.bfloat16)
-    queries = one_head[:, 0]
-    key_rows = one_head[:, 1]
-    value_rows = one_head[:, 2]
+    one_head = one_head.reshape(3, tokens, HEAD)
+    one_head = (one_head.astype(jnp.float32) * inverse_rms[None, :, None]).astype(jnp.bfloat16)
+    queries = (
+        one_head[0]
+        .reshape(sections, cp_count, own_rows, HEAD)
+        .transpose(1, 0, 2, 3)
+        .reshape(tokens, HEAD)
+    )
+    key_rows = one_head[1]
+    value_rows = one_head[2]
 
-    allowed = (sequence[:, None] == sequence[None, :]) & (position[None, :] <= position[:, None])
+    allowed = (query_sequence[:, None] == sequence[None, :]) & (
+        position[None, :] <= query_position[:, None]
+    )
     scores = jnp.dot(queries, key_rows.T, preferred_element_type=jnp.float32) / math.sqrt(HEAD)
     scores = jnp.where(allowed, scores, -1e30)
     row_peak = jnp.max(scores, axis=1, keepdims=True)

time: 394 us -> 348 us (0.88)
  local copies, waits for them, and re-layouts: 36 us -> 1.3 us
  other arithmetic: 37.1 us -> 18.3 us
  waiting for transfers between devices: 245 us -> 251 us
    reduce_scatter x1, waiting for transfers between devices: 25 us -> 46.7 us  [on_device(): one_head = lax.psum_scatter(partial, 'tp', scatter_dimension=0, tiled=True)]
    add x1 -> x2, other arithmetic: 15.8 us -> 0.14 us  [the longest x1 0.07 us: on_device(): packed_block.reshape(sections, cp_count).T.reshape(blocks)[:, None]]
    all_gather x1, waiting for transfers between devices: 86.4 us -> 70.8 us  [on_device(): lax.all_gather(rollout_rows, ('section', 'cp'), axis=0, tiled=True)]
    unnamed x10 -> x13, local copies, waits for them, and re-layouts: 13.6 us -> 0.82 us
    convert_element_type x1 -> x0, local copies, waits for them, and re-layouts: 11.3 us -> none  [on_device(): partial = jnp.einsum('rd,kdje->jrke', scaled, weights4, preferred_element...]
    another operation x1 -> x0, local copies, waits for them, and re-layouts: 9.73 us -> none  [on_device(): weights4 = qkv_weights.reshape(3, width_here, heads_here, HEAD)]
    gather x26 -> x0, other arithmetic: 6.27 us -> none  [on_device(): position = packed_block[actor_block] * own_rows + layout_rows % own_rows]
    dot_general x1 -> x4, matrix products: 18.6 us -> 22.6 us  [on_device(): jnp.einsum('rd,kde->kre', scaled, qkv_weights[:, :, j * HEAD:(j + 1) * HE...]
  transfers between devices with their start and end apart: 4 -> 4, of which waited for: 4 -> 4; matrix products, arithmetic and copies ran while one was open for 10% -> 2% of each run, Pallas kernels for 0% -> 0%
where the time goes in v2:
time: 348 us; the launch traced here: 347 us
  waiting for transfers between devices  251 us (72%)
  matrix products  41.6 us (12%)
  blocking collectives  21.5 us (6%)
  other arithmetic  18.3 us (5%)
  between operations  13.3 us (4%)
    reduce_scatter x1, waiting for transfers between devices, on_device(): lax.psum_scatter(partial_out, 'cp', scatter_dimension=0, tiled=True)  103 us
    all_gather x1, waiting for transfers between devices, on_device(): lax.all_gather(rollout_rows, ('section', 'cp'), axis=0, tiled=True)  70.8 us
    reduce_scatter x1, waiting for transfers between devices, on_device(): one_head = lax.psum_scatter(partial, 'tp', scatter_dimension=0, tiled=True)  46.7 us
    all_gather x1, waiting for transfers between devices, on_device(): group_att = lax.all_gather(attended, 'tp', axis=0, tiled=False)  30.3 us
    dot_general x4, matrix products, on_device(): jnp.einsum('rd,kde->kre', scaled, qkv_weights[:, :, j * HEAD:(j + 1) * HE...  22.6 us
    psum x1, blocking collectives, on_device(): total_squares = lax.psum(squares, 'tp')  11 us
    all_to_all x1, blocking collectives, on_device(): lax.all_to_all(branch, 'section', split_axis=0, concat_axis=0, tiled=True)  10.5 us
    dot_general x1, matrix products, on_device(): jnp.einsum('jre,jew->rw', group_att, out_weight, preferred_element_type=j...  8.36 us
  transfers between devices with their start and end apart: 4, of which 4 were waited for; matrix products, arithmetic and copies ran while one was open for 2% of the time, Pallas kernels for 0%

profile of v2, /device:TPU:0, one launch (start us, length us, event | category | flops | bytes accessed | tf_op | source)
XLA Modules:
  0.0 347.4 jit_solution(5885156782327738369)
XLA Ops:
  6.5 0.0 copy-start
  6.5 0.0 all-gather.4.cloned.1.call-start
  6.5 0.7 all-gather.4.cloned.1.call-update
  7.3 0.0 reduce-scatter.3.cloned.1.call-start
  7.3 70.8 %all-gather.4.cloned.1.call-done = bf16[2048,2048]{1,0:T(8,128)(2,1)} async-done(((bf16[64,2048]{1,0:T(8,128)(2,1)}), bf16[2048,2048]{1,0:T(8,128)(2,1)}) %all-gather.4.cloned.1.call-update) | async-done | bytes 8388624 | tf_op jit(solution)/shard_map/all_gather | solution.py:20
  78.1 0.0 copy-start.1
  78.1 0.0 copy-start.2
  78.1 0.0 copy-start.3
  78.1 8.5 %fusion.10 = bf16[1,3,2048,128]{3,2,1,0:T(8,128)(2,1)S(1)} fusion(bf16[3,2048,512]{2,1,0:T(8,128)(2,1)} %bitcast.58, bf16[2048,2048]{1,0:T(8,128)(2,1)} %all-gather.4.cloned.1.call-done, f32[2048]{0:T(1024)} %bitcast.63), kind=kOutput, calls=%fused_computation.21 | convolution fusion | flops 3234594816 | bytes 11542528 | tf_op jit(solution)/shard_map/rd,kde->kre/dot_general | solution.py:48
  86.6 0.0 copy-done.1
  86.6 0.0 copy-done.2
  86.6 0.0 copy-done.3
  86.6 4.6 %fusion.11 = bf16[1,3,2048,128]{3,2,1,0:T(8,128)(2,1)S(1)} fusion(bf16[3,2048,512]{2,1,0:T(8,128)(2,1)S(1)} %bitcast.59, bf16[2048,2048]{1,0:T(8,128)(2,1)S(1)} %copy-done.1, f32[2048]{0:T(1024)S(1)} %bitcast.64), kind=kOutput, calls=%fused_computation.22 | convolution fusion | flops 3234594816 | bytes 11542528 | tf_op jit(solution)/shard_map/rd,kde->kre/dot_general | solution.py:48
  91.3 4.8 %fusion.12 = bf16[1,3,2048,128]{3,2,1,0:T(8,128)(2,1)S(1)} fusion(bf16[3,2048,512]{2,1,0:T(8,128)(2,1)S(1)} %bitcast.60, bf16[2048,2048]{1,0:T(8,128)(2,1)S(1)} %copy-done.1, f32[2048]{0:T(1024)S(1)} %bitcast.65), kind=kOutput, calls=%fused_computation.23 | convolution fusion | flops 3234594816 | bytes 11542528 | tf_op jit(solution)/shard_map/rd,kde->kre/dot_general | solution.py:48
  96.1 4.6 %fusion.9 = bf16[1,3,2048,128]{3,2,1,0:T(8,128)(2,1)S(1)} fusion(bf16[3,2048,512]{2,1,0:T(8,128)(2,1)S(1)} %bitcast.61, bf16[2048,2048]{1,0:T(8,128)(2,1)S(1)} %copy-done.1, f32[2048]{0:T(1024)S(1)} %bitcast.66), kind=kOutput, calls=%fused_computation.20 | convolution fusion | flops 3234594816 | bytes 11542528 | tf_op jit(solution)/shard_map/rd,kde->kre/dot_general | solution.py:48
  100.7 0.0 copy-start.4
  100.8 0.0 copy-start.5
  100.8 3.3 pad_maximum_fusion
  104.1 0.0 reduce-scatter.3.cloned.1.call-update
  104.1 0.0 all-gather.6.cloned.1.call-start
  104.1 0.0 copy-done.4
  104.1 0.1 select_reduce_fusion
  104.3 0.1 mul.42
  104.3 0.1 copy.11
  104.4 0.1 mul.44
  104.5 0.1 iota_add_fusion.1
  104.6 0.1 add.59
  104.7 0.1 iota_add_fusion
  104.7 0.1 add.63
  104.8 0.0 copy-done.5
  104.8 0.2 reduce-window.8
  105.0 0.1 fusion.25
  105.1 5.1 %fusion.1 = f32[2048]{0:T(1024)S(1)} fusion(bf16[2048,2048]{1,0:T(8,128)(2,1)} %all-gather.4.cloned.1.call-done), kind=kLoop, calls=%fused_computation.3 | loop fusion | flops 12580864 | bytes 8396800 | tf_op jit(solution)/shard_map/reduce_sum | solution.py:38
  110.2 11.0 %psum.7 = f32[2048]{0:T(1024)S(1)} all-reduce(f32[2048]{0:T(1024)S(1)} %fusion.1), channel_id=1, replica_groups=mesh['section'=2,'cp'=16,'tp'=4] {'tp'}, use_global_device_ids=true, to_apply=%region_6.7 | all-reduce | flops 2048 | bytes 16384 | tf_op jit(solution)/shard_map/psum | solution.py:39
  121.2 46.7 %reduce-scatter.3.cloned.1.call-done = bf16[6144,128]{1,0:T(8,128)(2,1)} async-done(((bf16[24576,128]{1,0:T(8,128)(2,1)}), bf16[6144,128]{1,0:T(8,128)(2,1)}) %reduce-scatter.3.cloned.1.call-update) | async-done | bytes 1572880 | tf_op jit(solution)/shard_map/reduce_scatter | solution.py:58
  167.9 1.9 fusion.8
  169.9 4.0 %fusion.2 = (f32[2048]{0:T(1024)S(1)}, f32[2048,2048]{0,1:T(8,128)S(1)}) fusion(s32[2048]{0:T(1024)S(1)} %add.59, s32[2048]{0:T(1024)S(1)} %get-tuple-element.6, s32[2048]{0:T(1024)S(1)} %add.63, s32[2048]{0:T(1024)S(1)} %get-tuple-element.5, bf16[2048,128]{1,0:T(8,128)(2,1)S(1)} %bitcast.55, bf16[3,2048,128]{2,1,0:T(8,128)(2,1)S(1)} %fusion.8), kind=kOutput, calls=%fused_computation.8 | convolution fusion | flops 1098905600 | bytes 17866752 | tf_op jit(solution)/shard_map/dot_general | solution.py:73
  173.9 7.5 %fusion.3 = f32[2048]{0:T(1024)S(1)} fusion(f32[2048,2048]{0,1:T(8,128)S(1)} %get-tuple-element.8, f32[2048]{0:T(1024)S(1)} %get-tuple-element.7, s32[2048]{0:T(1024)S(1)} %add.59, s32[2048]{0:T(1024)S(1)} %get-tuple-element.6, s32[2048]{0:T(1024)S(1)} %add.63, s32[2048]{0:T(1024)S(1)} %get-tuple-element.5), kind=kLoop, calls=%fused_computation.9 | loop fusion | flops 33552384 | bytes 16826368 | tf_op jit(solution)/shard_map/reduce_sum | solution.py:77
  181.4 6.6 %fusion.16 = bf16[2048,128]{1,0:T(8,128)(2,1)} fusion(f32[2048,2048]{0,1:T(8,128)S(1)} %get-tuple-element.8, f32[2048]{0:T(1024)S(1)} %get-tuple-element.7, s32[2048]{0:T(1024)S(1)} %add.59, s32[2048]{0:T(1024)S(1)} %get-tuple-element.6, s32[2048]{0:T(1024)S(1)} %add.63, s32[2048]{0:T(1024)S(1)} %get-tuple-element.5, bf16[3,2048,128]{2,1,0:T(8,128)(2,1)S(1)} %fusion.8, ...), kind=kOutput, calls=%fused_computation.25 | convolution fusion | flops 1107820544 | bytes 17874944 | tf_op jit(solution)/shard_map/dot_general | solution.py:79
  188.0 0.0 all-gather.6.cloned.1.call-update
  188.0 0.0 reduce-scatter.5.cloned.1.call-start
  188.1 30.3 %all-gather.6.cloned.1.call-done = bf16[8192,128]{1,0:T(8,128)(2,1)} async-done(((bf16[2048,128]{1,0:T(8,128)(2,1)}), bf16[8192,128]{1,0:T(8,128)(2,1)}) %all-gather.6.cloned.1.call-update) | async-done | bytes 2097168 | tf_op jit(solution)/shard_map/all_gather | solution.py:82
  218.4 0.0 copy-done
  218.4 8.4 %bitcast_convert_fusion = bf16[2048,2048]{1,0:T(8,128)(2,1)} fusion(bf16[4,2048,128]{2,1,0:T(8,128)(2,1)} %bitcast.62, bf16[4,128,2048]{2,1,0:T(8,128)(2,1)S(1)} %bitcast.50), kind=kOutput, calls=%fused_computation.4 | convolution fusion | flops 4299161600 | bytes 12582912 | tf_op jit(solution)/shard_map/jre,jew->rw/dot_general | solution.py:84
  226.8 0.0 reduce-scatter.5.cloned.1.call-update
  226.8 102.8 %reduce-scatter.5.cloned.1.call-done = bf16[128,2048]{1,0:T(8,128)(2,1)} async-done(((bf16[2048,2048]{1,0:T(8,128)(2,1)}), bf16[128,2048]{1,0:T(8,128)(2,1)}) %reduce-scatter.5.cloned.1.call-update) | async-done | bytes 524304 | tf_op jit(solution)/shard_map/reduce_scatter | solution.py:87
  329.6 10.5 %all_to_all.5 = bf16[2,64,2048]{2,1,0:T(8,128)(2,1)S(1)} all-to-all(bf16[2,64,2048]{2,1,0:T(8,128)(2,1)} %bitcast.54), channel_id=1, replica_groups=mesh['section'=2,'cp'=16,'tp'=4] {'section'}, dimensions={0} | all-to-all | bytes 1048576 | tf_op jit(solution)/shard_map/all_to_all | solution.py:89
  340.1 0.8 copy.14
  (4 shorter events, 0.1 us)
Async XLA Ops:
  6.5 211.9 %copy-start = (bf16[1,512,2048]{2,1,0:T(8,128)(2,1)S(1)}, bf16[1,512,2048]{2,1,0:T(8,128)(2,1)}, u32[]{:S(2)}) copy-start(bf16[1,512,2048]{2,1,0:T(8,128)(2,1)} %param.11) | copy-start | bytes 6291460
  6.5 71.5 %all-gather.4.cloned.1.call-start = ((), (), s32[]{:S(2)}) async-start(), calls=%async_computation.3 | async-start | bytes 8650752 | tf_op jit(solution)/shard_map/all_gather | solution.py:20
  7.3 160.6 %reduce-scatter.3.cloned.1.call-start = ((), (), s32[]{:S(2)}) async-start(), calls=%async_computation.4 | async-start | bytes 7864320 | tf_op jit(solution)/shard_map/reduce_scatter | solution.py:58
  78.1 8.5 %copy-start.1 = (bf16[2048,2048]{1,0:T(8,128)(2,1)S(1)}, bf16[2048,2048]{1,0:T(8,128)(2,1)}, u32[]{:S(2)}) copy-start(bf16[2048,2048]{1,0:T(8,128)(2,1)} %all-gather.4.cloned.1.call-done) | copy-start | bytes 25165828
  78.1 8.5 %copy-start.2 = (bf16[1,3,2048,512]{3,2,1,0:T(8,128)(2,1)S(1)}, bf16[1,3,2048,512]{3,2,1,0:T(8,128)(2,1)}, u32[]{:S(2)}) copy-start(bf16[1,3,2048,512]{3,2,1,0:T(8,128)(2,1)} %param.10) | copy-start | bytes 18874372
  78.1 8.5 %copy-start.3 = (f32[1,2048]{1,0:T(1,128)S(1)}, f32[1,2048]{1,0:T(1,128)}, u32[]{:S(2)}) copy-start(f32[1,2048]{1,0:T(1,128)} %param.9) | copy-start | bytes 24580
  100.7 3.4 copy-start.4
  100.8 4.1 %copy-start.5 = (s32[2]{0:T(128)S(1)}, s32[2]{0:T(128)}, u32[]{:S(2)}) copy-start(s32[2]{0:T(128)} %param.7) | copy-start | bytes 28
  104.1 114.3 %all-gather.6.cloned.1.call-start = ((), (), s32[]{:S(2)}) async-start(), calls=%async_computation.6 | async-start | bytes 2621440 | tf_op jit(solution)/shard_map/all_gather | solution.py:82
  188.0 141.6 %reduce-scatter.5.cloned.1.call-start = ((), (), s32[]{:S(2)}) async-start(), calls=%async_computation.5 | async-start | bytes 8912896 | tf_op jit(solution)/shard_map/reduce_scatter | solution.py:87
Sparse Core Ops, SparseCore 0:
  9.1 68.9 all-gather.3
  104.2 63.6 reduce-scatter.2
  188.2 30.1 all-gather.5
  226.9 102.6 reduce-scatter.4

commit v3 on v2

--- a/solution.py
+++ b/solution.py
@@ -7,6 +7,10 @@
 
 D = 8192
 HEAD = 128
+
+
+def shifted(value, axis, count, step):
+    return lax.ppermute(value, axis, perm=[(j, (j + step) % count) for j in range(count)])
 
 
 def on_device(rollout_rows, lengths, block_owner, norm_gain, w_qkv, w_out):
@@ -34,30 +38,26 @@
         (query_position[:, None] >= seq_ends[None, :]).astype(jnp.int32), axis=1
     )
 
+    me_tp = lax.axis_index("tp")
     rows_f32 = rows_in.astype(jnp.float32)
     squares = jnp.sum(jnp.square(rows_f32), axis=1)
-    total_squares = lax.psum(squares, "tp")
+    total_squares = squares
+    for step in range(1, tp_count):
+        total_squares = total_squares + shifted(squares, "tp", tp_count, step)
     inverse_rms = lax.rsqrt(total_squares / D + 1e-05)
     scaled = (rows_f32 * norm_gain[0][None, :]).astype(jnp.bfloat16)
 
     qkv_weights = w_qkv[0]
-    group_cols = qkv_weights.shape[2]
-    heads_here = group_cols // HEAD
-    partial = jnp.stack(
-        [
-            jnp.einsum(
-                "rd,kde->kre",
-                scaled,
-                qkv_weights[:, :, j * HEAD : (j + 1) * HEAD],
-                preferred_element_type=jnp.float32,
-            ).astype(jnp.bfloat16)
-            for j in range(heads_here)
-        ]
-    )
-    partial = partial.reshape(heads_here * 3 * tokens, HEAD)
-    one_head = lax.psum_scatter(partial, "tp", scatter_dimension=0, tiled=True)
-    one_head = one_head.reshape(3, tokens, HEAD)
-    one_head = (one_head.astype(jnp.float32) * inverse_rms[None, :, None]).astype(jnp.bfloat16)
+
+    def head_partial(head):
+        head_weights = lax.dynamic_slice_in_dim(qkv_weights, head * HEAD, HEAD, axis=2)
+        return jnp.einsum("rd,kde->kre", scaled, head_weights, preferred_element_type=jnp.float32)
+
+    summed = head_partial(me_tp)
+    for step in range(1, tp_count):
+        piece = head_partial((me_tp + step) % tp_count).astype(jnp.bfloat16)
+        summed = summed + shifted(piece, "tp", tp_count, step).astype(jnp.float32)
+    one_head = (summed * inverse_rms[None, :, None]).astype(jnp.bfloat16)
     queries = (
         one_head[0]
         .reshape(sections, cp_count, own_rows, HEAD)
@@ -79,13 +79,15 @@
     mixed = jnp.dot(probabilities, value_rows, preferred_element_type=jnp.float32)
     attended = (mixed / row_total).astype(jnp.bfloat16)
 
-    group_att = lax.all_gather(attended, "tp", axis=0, tiled=False)
+    parts = [attended] + [shifted(attended, "tp", tp_count, step) for step in range(1, tp_count)]
     out_weight = w_out[0].reshape(tp_count, HEAD, width_here)
+    source_of = (me_tp - jnp.arange(tp_count, dtype=jnp.int32)) % tp_count
+    out_weight = jnp.take(out_weight, source_of, axis=0)
     partial_out = jnp.einsum(
-        "jre,jew->rw", group_att, out_weight, preferred_element_type=jnp.float32
+        "kre,kew->rw", jnp.stack(parts), out_weight, preferred_element_type=jnp.float32
     ).astype(jnp.bfloat16)
-    summed = lax.psum_scatter(partial_out, "cp", scatter_dimension=0, tiled=True)
-    branch = summed.reshape(sections, own_rows, width_here)
+    reduced = lax.psum_scatter(partial_out, "cp", scatter_dimension=0, tiled=True)
+    branch = reduced.reshape(sections, own_rows, width_here)
     return lax.all_to_all(branch, "section", split_axis=0, concat_axis=0, tiled=True)
 
 

time: 348 us -> 351 us (level)
  starting transfers between devices: 0.12 us -> 16.6 us
  blocking collectives: 21.5 us -> 10.7 us
  waiting for transfers between devices: 251 us -> 243 us
  matrix products: 41.6 us -> 48.4 us
  other arithmetic: 18.3 us -> 13.8 us
    ppermute x0 -> x9, waiting for transfers between devices: none -> 70.5 us  [shifted(): lax.ppermute(value, axis, perm=[(j, (j + step) % count) for j in range(co...]
    reduce_scatter x1 -> x0, waiting for transfers between devices: 46.7 us -> none  [on_device(): one_head = lax.psum_scatter(partial, 'tp', scatter_dimension=0, tiled=True)]
    all_gather x1 -> x0, waiting for transfers between devices: 30.3 us -> none  [on_device(): group_att = lax.all_gather(attended, 'tp', axis=0, tiled=False)]
    ppermute x0 -> x9, starting transfers between devices: none -> 16.5 us  [shifted(): lax.ppermute(value, axis, perm=[(j, (j + step) % count) for j in range(co...]
    psum x1 -> x0, blocking collectives: 11 us -> none  [on_device(): total_squares = lax.psum(squares, 'tp')]
    dot_general x5, matrix products: 31 us -> 35.7 us  [the longest x4 27.2 us: head_partial(): jnp.einsum('rd,kde->kre', scaled, head_weights, preferred_element_type=jn...]
  transfers between devices with their start and end apart: 4 -> 11, of which waited for: 4 -> 6; matrix products, arithmetic and copies ran while one was open for 2% -> 5% of each run, Pallas kernels for 0% -> 0%
where the time goes in v3:
time: 351 us
  waiting for transfers between devices  243 us (69%)
  matrix products  48.4 us (14%)
  starting transfers between devices  16.6 us (5%)
  other arithmetic  13.8 us (4%)
  between operations  13.6 us (4%)
  blocking collectives  10.7 us (3%)
  local copies, waits for them, and re-layouts  4.78 us (1%)
    reduce_scatter x1, waiting for transfers between devices, on_device(): lax.psum_scatter(partial_out, 'cp', scatter_dimension=0, tiled=True)  102 us
    ppermute x9, waiting for transfers between devices, shifted(): lax.ppermute(value, axis, perm=[(j, (j + step) % count) for j in range(co...  70.5 us
    all_gather x1, waiting for transfers between devices, on_device(): lax.all_gather(rollout_rows, ('section', 'cp'), axis=0, tiled=True)  70 us
    dot_general x4, matrix products, head_partial(): jnp.einsum('rd,kde->kre', scaled, head_weights, preferred_element_type=jn...  27.2 us
    ppermute x9, starting transfers between devices, shifted(): lax.ppermute(value, axis, perm=[(j, (j + step) % count) for j in range(co...  16.5 us
    all_to_all x1, blocking collectives, on_device(): lax.all_to_all(branch, 'section', split_axis=0, concat_axis=0, tiled=True)  10.7 us
    dot_general x1, matrix products, on_device(): jnp.einsum('kre,kew->rw', jnp.stack(parts), out_weight, preferred_element...  8.45 us
    reduce_sum x1, other arithmetic, on_device(): row_total = jnp.sum(weights, axis=1, keepdims=True)  7.45 us
  transfers between devices with their start and end apart: 11, of which 6 were waited for; matrix products, arithmetic and copies ran while one was open for 5% of the time, Pallas kernels for 0%

profile of v3, /device:TPU:0, one launch (start us, length us, event | category | flops | bytes accessed | tf_op | source)
XLA Modules:
  0.0 350.9 jit_solution(267863916217169514)
XLA Ops:
  6.5 0.0 copy-start
  6.5 0.0 all-gather.2.cloned.1.call-start
  6.5 0.7 all-gather.2.cloned.1.call-update
  7.3 0.0 reduce-scatter.2.cloned.1.call-start
  7.4 0.8 select_reduce_fusion
  8.1 70.0 %all-gather.2.cloned.1.call-done = bf16[2048,2048]{1,0:T(8,128)(2,1)} async-done(((bf16[64,2048]{1,0:T(8,128)(2,1)}), bf16[2048,2048]{1,0:T(8,128)(2,1)}) %all-gather.2.cloned.1.call-update) | async-done | bytes 8388624 | tf_op jit(solution)/shard_map/all_gather | solution.py:24
  78.1 0.0 copy-start.1
  78.1 0.0 copy-start.3
  78.1 0.0 copy-start.4
  78.1 8.6 %fusion.12 = bf16[3,2048,128]{1,2,0:T(8,128)(2,1)} fusion(bf16[1,3,2048,512]{3,2,1,0:T(8,128)(2,1)} %param.10, s32[]{:T(128)S(6)} %select_n.78, bf16[2048,2048]{1,0:T(8,128)(2,1)} %all-gather.2.cloned.1.call-done, f32[2048]{0:T(1024)} %bitcast.75), kind=kOutput, calls=%fused_computation.22 | convolution fusion | flops 3234594816 | bytes 11542532 | tf_op jit(solution)/shard_map/rd,kde->kre/dot_general | solution.py:54
  86.6 1.5 collective-permute-start
  88.1 0.0 copy-done.1
  88.1 0.0 copy-done.3
  88.1 0.0 copy-done.4
  88.1 4.8 %fusion.13 = bf16[3,2048,128]{1,2,0:T(8,128)(2,1)} fusion(bf16[1,3,2048,512]{3,2,1,0:T(8,128)(2,1)S(1)} %copy-done.3, s32[]{:T(128)S(6)} %select_n.80, bf16[2048,2048]{1,0:T(8,128)(2,1)S(1)} %copy-done.1, f32[2048]{0:T(1024)S(1)} %bitcast.76), kind=kOutput, calls=%fused_computation.23 | convolution fusion | flops 3234594816 | bytes 11542532 | tf_op jit(solution)/shard_map/rd,kde->kre/dot_general | solution.py:54
  92.9 2.5 collective-permute-start.1
  95.4 4.7 %fusion.14 = bf16[3,2048,128]{1,2,0:T(8,128)(2,1)} fusion(bf16[1,3,2048,512]{3,2,1,0:T(8,128)(2,1)S(1)} %copy-done.3, s32[]{:T(128)S(6)} %select_n.82, bf16[2048,2048]{1,0:T(8,128)(2,1)S(1)} %copy-done.1, f32[2048]{0:T(1024)S(1)} %bitcast.77), kind=kOutput, calls=%fused_computation.24 | convolution fusion | flops 3234594816 | bytes 11542532 | tf_op jit(solution)/shard_map/rd,kde->kre/dot_general | solution.py:54
  100.1 0.0 copy-start.5
  100.1 1.6 collective-permute-start.2
  101.8 0.1 mul.54
  101.9 0.1 copy.19
  101.9 0.1 mul.56
  102.0 0.1 iota_add_fusion
  102.1 5.1 %fusion.1 = f32[2048]{0:T(1024)S(1)} fusion(bf16[2048,2048]{1,0:T(8,128)(2,1)} %all-gather.2.cloned.1.call-done), kind=kLoop, calls=%fused_computation.4 | loop fusion | flops 12580864 | bytes 8396800 | tf_op jit(solution)/shard_map/reduce_sum | solution.py:43
  107.2 0.5 collective-permute-start.3
  107.6 0.1 iota_add_fusion.1
  107.7 0.1 add.136
  107.8 0.1 add.140
  107.9 0.0 copy-done.5
  107.9 0.2 reduce-window.8
  108.0 1.1 collective-permute-start.4
  109.1 47.3 %collective-permute-done.3 = f32[2048]{0:T(1024)S(1)} collective-permute-done((f32[2048]{0:T(1024)S(1)}, f32[2048]{0:T(1024)S(1)}, u32[]{:S(2)}, u32[]{:S(2)}) %collective-permute-start.3) | collective-permute-done | bytes 8224 | tf_op jit(solution)/shard_map/ppermute | solution.py:13
  156.4 3.6 %collective-permute-start.5 = (f32[2048]{0:T(1024)S(1)}, f32[2048]{0:T(1024)S(1)}, u32[]{:S(2)}, u32[]{:S(2)}) collective-permute-start(f32[2048]{0:T(1024)S(1)} %fusion.1), channel_id=1, source_target_pairs={{0,3},{1,0},{2,1},{3,2},{4,7},{5,4},{6,5},{7,6},{8,11},{9,8},{10,9... | collective-permute-start | bytes 24584 | tf_op jit(solution)/shard_map/ppermute | solution.py:13
  160.0 0.1 fusion.44
  160.1 0.0 collective-permute-done.4
  160.1 3.8 %collective-permute-done.5 = f32[2048]{0:T(1024)S(1)} collective-permute-done((f32[2048]{0:T(1024)S(1)}, f32[2048]{0:T(1024)S(1)}, u32[]{:S(2)}, u32[]{:S(2)}) %collective-permute-start.5) | collective-permute-done | bytes 8224 | tf_op jit(solution)/shard_map/ppermute | solution.py:13
  163.9 0.0 collective-permute-done
  164.0 0.0 collective-permute-done.1
  164.0 0.0 collective-permute-done.2
  164.0 9.2 %fusion.11 = bf16[3,2048,128]{1,2,0:T(8,128)(2,1)S(1)} fusion(bf16[3,2048,128]{1,2,0:T(8,128)(2,1)} %collective-permute-done.2, bf16[3,2048,128]{1,2,0:T(8,128)(2,1)} %collective-permute-done.1, bf16[3,2048,128]{1,2,0:T(8,128)(2,1)} %collective-permute-done, f32[2048]{0:T(1024)S(1)} %add_rsqrt_fusion, bf16[1,3,2048,512]{3,2,1,0:T(8,128)(2,1)} %param.10, ...), kind=kOutput, calls=%fused_computation.18 | convolution fusion | flops 3240099840 | bytes 16269316 | tf_op jit(solution)/shard_map/rd,kde->kre/dot_general | solution.py:54
  173.2 0.0 copy-start.2
  173.2 1.1 copy-done.2
  174.4 0.3 copy.24
  174.7 5.7 %fusion.2 = (f32[2048]{0:T(1024)S(1)}, f32[2048,2048]{0,1:T(8,128)S(1)}) fusion(s32[2048]{0:T(1024)S(1)} %add.136, s32[2048]{0:T(1024)S(1)} %get-tuple-element.6, s32[2048]{0:T(1024)S(1)} %add.140, s32[2048]{0:T(1024)S(1)} %get-tuple-element.5, bf16[2048,128]{1,0:T(8,128)(2,1)S(1)} %bitcast.70, bf16[3,2048,128]{1,2,0:T(8,128)(2,1)} %copy-done.2), kind=kOutput, calls=%fused_computation.9 | convolution fusion | flops 1098905600 | bytes 17866752 | tf_op jit(solution)/shard_map/dot_general | solution.py:73
  180.4 7.4 %fusion.3 = f32[2048]{0:T(1024)S(1)} fusion(f32[2048,2048]{0,1:T(8,128)S(1)} %get-tuple-element.8, f32[2048]{0:T(1024)S(1)} %get-tuple-element.7, s32[2048]{0:T(1024)S(1)} %add.136, s32[2048]{0:T(1024)S(1)} %get-tuple-element.6, s32[2048]{0:T(1024)S(1)} %add.140, s32[2048]{0:T(1024)S(1)} %get-tuple-element.5), kind=kLoop, calls=%fused_computation.10 | loop fusion | flops 33552384 | bytes 16826368 | tf_op jit(solution)/shard_map/reduce_sum | solution.py:77
  187.9 7.0 %fusion.27 = bf16[2048,128]{1,0:T(8,128)(2,1)S(1)} fusion(f32[2048,2048]{0,1:T(8,128)S(1)} %get-tuple-element.8, f32[2048]{0:T(1024)S(1)} %get-tuple-element.7, s32[2048]{0:T(1024)S(1)} %add.136, s32[2048]{0:T(1024)S(1)} %get-tuple-element.6, s32[2048]{0:T(1024)S(1)} %add.140, s32[2048]{0:T(1024)S(1)} %get-tuple-element.5, ...), kind=kOutput, calls=%fused_computation.35 | convolution fusion | flops 1107820544 | bytes 17874944 | tf_op jit(solution)/shard_map/dot_general | solution.py:79
  194.9 2.5 collective-permute-start.6
  197.4 1.6 collective-permute-start.7
  199.1 1.6 collective-permute-start.8
  200.7 0.0 copy-done
  200.8 2.1 gather_fusion
  202.8 6.9 %collective-permute-done.6 = bf16[2048,128]{1,0:T(8,128)(2,1)S(1)} collective-permute-done((bf16[2048,128]{1,0:T(8,128)(2,1)S(1)}, bf16[2048,128]{1,0:T(8,128)(2,1)S(1)}, u32[]{:S(2)}, u32[]{:S(2)}) %collective-permute-start.6) | collective-permute-done | bytes 524320 | tf_op jit(solution)/shard_map/ppermute | solution.py:13
  209.7 12.5 %collective-permute-done.7 = bf16[2048,128]{1,0:T(8,128)(2,1)} collective-permute-done((bf16[2048,128]{1,0:T(8,128)(2,1)S(1)}, bf16[2048,128]{1,0:T(8,128)(2,1)}, u32[]{:S(2)}, u32[]{:S(2)}) %collective-permute-start.7) | collective-permute-done | bytes 524320 | tf_op jit(solution)/shard_map/ppermute | solution.py:13
  222.2 0.0 collective-permute-done.8
  222.3 8.5 %bitcast_convert_fusion = bf16[2048,2048]{1,0:T(8,128)(2,1)} fusion(bf16[1,2048,128]{2,1,0:T(8,128)(2,1)} %bitcast.21, bf16[1,2048,128]{2,1,0:T(8,128)(2,1)} %bitcast.20, bf16[1,2048,128]{2,1,0:T(8,128)(2,1)S(1)} %bitcast.74, bf16[1,2048,128]{2,1,0:T(8,128)(2,1)S(1)} %bitcast.73, bf16[4,128,2048]{2,1,0:T(8,128)(2,1)} %gather_fusion, ...), kind=kOutput, calls=%fused_computation.5 | convolution fusion | flops 4303355904 | bytes 12582916 | tf_op jit(solution)/shard_map/kre,kew->rw/dot_general | solution.py:86
  230.7 0.0 reduce-scatter.2.cloned.1.call-update
  230.7 101.9 %reduce-scatter.2.cloned.1.call-done = bf16[128,2048]{1,0:T(8,128)(2,1)} async-done(((bf16[2048,2048]{1,0:T(8,128)(2,1)}), bf16[128,2048]{1,0:T(8,128)(2,1)}) %reduce-scatter.2.cloned.1.call-update) | async-done | bytes 524304 | tf_op jit(solution)/shard_map/reduce_scatter | solution.py:89
  332.6 10.7 %all_to_all.5 = bf16[2,64,2048]{2,1,0:T(8,128)(2,1)S(1)} all-to-all(bf16[2,64,2048]{2,1,0:T(8,128)(2,1)} %bitcast.69), channel_id=1, replica_groups=mesh['section'=2,'cp'=16,'tp'=4] {'section'}, dimensions={0} | all-to-all | bytes 1048576 | tf_op jit(solution)/shard_map/all_to_all | solution.py:91
  343.3 0.8 copy.27
  (7 shorter events, 0.1 us)
Async XLA Ops:
  6.5 194.2 %copy-start = (bf16[1,512,2048]{2,1,0:T(8,128)(2,1)S(1)}, bf16[1,512,2048]{2,1,0:T(8,128)(2,1)}, u32[]{:S(2)}) copy-start(bf16[1,512,2048]{2,1,0:T(8,128)(2,1)} %param.11) | copy-start | bytes 6291460
  6.5 71.5 %all-gather.2.cloned.1.call-start = ((), (), s32[]{:S(2)}) async-start(), calls=%async_computation.2 | async-start | bytes 8650752 | tf_op jit(solution)/shard_map/all_gather | solution.py:24
  7.3 325.3 %reduce-scatter.2.cloned.1.call-start = ((), (), s32[]{:S(2)}) async-start(), calls=%async_computation.3 | async-start | bytes 8912896 | tf_op jit(solution)/shard_map/reduce_scatter | solution.py:89
  78.1 10.0 %copy-start.1 = (bf16[2048,2048]{1,0:T(8,128)(2,1)S(1)}, bf16[2048,2048]{1,0:T(8,128)(2,1)}, u32[]{:S(2)}) copy-start(bf16[2048,2048]{1,0:T(8,128)(2,1)} %all-gather.2.cloned.1.call-done) | copy-start | bytes 25165828
  78.1 10.0 %copy-start.3 = (bf16[1,3,2048,512]{3,2,1,0:T(8,128)(2,1)S(1)}, bf16[1,3,2048,512]{3,2,1,0:T(8,128)(2,1)}, u32[]{:S(2)}) copy-start(bf16[1,3,2048,512]{3,2,1,0:T(8,128)(2,1)} %param.10) | copy-start | bytes 18874372
  78.1 10.0 %copy-start.4 = (f32[1,2048]{1,0:T(1,128)S(1)}, f32[1,2048]{1,0:T(1,128)}, u32[]{:S(2)}) copy-start(f32[1,2048]{1,0:T(1,128)} %param.9) | copy-start | bytes 24580
  86.6 77.3 %collective-permute-start = (bf16[3,2048,128]{1,2,0:T(8,128)(2,1)}, bf16[3,2048,128]{1,2,0:T(8,128)(2,1)}, u32[]{:S(2)}, u32[]{:S(2)}) collective-permute-start(bf16[3,2048,128]{1,2,0:T(8,128)(2,1)} %fusion.12), channel_id=1, source_target_pairs={{0,1},{1,2},{2,3},{3,0},{4,5},{5,6},{6,7},{7,4},{8,9},{9,10},{10,1... | collective-permute-start | bytes 4718600 | tf_op jit(solution)/shard_map/ppermute | solution.py:13
  92.9 71.1 %collective-permute-start.1 = (bf16[3,2048,128]{1,2,0:T(8,128)(2,1)}, bf16[3,2048,128]{1,2,0:T(8,128)(2,1)}, u32[]{:S(2)}, u32[]{:S(2)}) collective-permute-start(bf16[3,2048,128]{1,2,0:T(8,128)(2,1)} %fusion.13), channel_id=1, source_target_pairs={{0,2},{1,3},{2,0},{3,1},{4,6},{5,7},{6,4},{7,5},{8,10},{9,11},{10,... | collective-permute-start | bytes 4718600 | tf_op jit(solution)/shard_map/ppermute | solution.py:13
  100.1 7.7 %copy-start.5 = (s32[2]{0:T(128)S(1)}, s32[2]{0:T(128)}, u32[]{:S(2)}) copy-start(s32[2]{0:T(128)} %param.7) | copy-start | bytes 28
  100.1 63.8 %collective-permute-start.2 = (bf16[3,2048,128]{1,2,0:T(8,128)(2,1)}, bf16[3,2048,128]{1,2,0:T(8,128)(2,1)}, u32[]{:S(2)}, u32[]{:S(2)}) collective-permute-start(bf16[3,2048,128]{1,2,0:T(8,128)(2,1)} %fusion.14), channel_id=1, source_target_pairs={{0,3},{1,0},{2,1},{3,2},{4,7},{5,4},{6,5},{7,6},{8,11},{9,8},{10,9... | collective-permute-start | bytes 4718600 | tf_op jit(solution)/shard_map/ppermute | solution.py:13
  107.2 49.2 %collective-permute-start.3 = (f32[2048]{0:T(1024)S(1)}, f32[2048]{0:T(1024)S(1)}, u32[]{:S(2)}, u32[]{:S(2)}) collective-permute-start(f32[2048]{0:T(1024)S(1)} %fusion.1), channel_id=1, source_target_pairs={{0,1},{1,2},{2,3},{3,0},{4,5},{5,6},{6,7},{7,4},{8,9},{9,10},{10,1... | collective-permute-start | bytes 24584 | tf_op jit(solution)/shard_map/ppermute | solution.py:13
  108.0 52.1 %collective-permute-start.4 = (f32[2048]{0:T(1024)S(1)}, f32[2048]{0:T(1024)S(1)}, u32[]{:S(2)}, u32[]{:S(2)}) collective-permute-start(f32[2048]{0:T(1024)S(1)} %fusion.1), channel_id=1, source_target_pairs={{0,2},{1,3},{2,0},{3,1},{4,6},{5,7},{6,4},{7,5},{8,10},{9,11},{10,... | collective-permute-start | bytes 24584 | tf_op jit(solution)/shard_map/ppermute | solution.py:13
  156.4 7.5 %collective-permute-start.5 = (f32[2048]{0:T(1024)S(1)}, f32[2048]{0:T(1024)S(1)}, u32[]{:S(2)}, u32[]{:S(2)}) collective-permute-start(f32[2048]{0:T(1024)S(1)} %fusion.1), channel_id=1, source_target_pairs={{0,3},{1,0},{2,1},{3,2},{4,7},{5,4},{6,5},{7,6},{8,11},{9,8},{10,9... | collective-permute-start | bytes 24584 | tf_op jit(solution)/shard_map/ppermute | solution.py:13
  173.2 1.2 copy-start.2
  194.9 14.8 %collective-permute-start.6 = (bf16[2048,128]{1,0:T(8,128)(2,1)S(1)}, bf16[2048,128]{1,0:T(8,128)(2,1)S(1)}, u32[]{:S(2)}, u32[]{:S(2)}) collective-permute-start(bf16[2048,128]{1,0:T(8,128)(2,1)S(1)} %fusion.27), channel_id=1, source_target_pairs={{0,1},{1,2},{2,3},{3,0},{4,5},{5,6},{6,7},{7,4},{8,9},{9,10},{10,1... | collective-permute-start | bytes 1572872 | tf_op jit(solution)/shard_map/ppermute | solution.py:13
  197.4 24.8 %collective-permute-start.7 = (bf16[2048,128]{1,0:T(8,128)(2,1)S(1)}, bf16[2048,128]{1,0:T(8,128)(2,1)}, u32[]{:S(2)}, u32[]{:S(2)}) collective-permute-start(bf16[2048,128]{1,0:T(8,128)(2,1)S(1)} %fusion.27), channel_id=1, source_target_pairs={{0,2},{1,3},{2,0},{3,1},{4,6},{5,7},{6,4},{7,5},{8,10},{9,11},{10,... | collective-permute-start | bytes 1572872 | tf_op jit(solution)/shard_map/ppermute | solution.py:13
  199.1 23.2 %collective-permute-start.8 = (bf16[2048,128]{1,0:T(8,128)(2,1)S(1)}, bf16[2048,128]{1,0:T(8,128)(2,1)}, u32[]{:S(2)}, u32[]{:S(2)}) collective-permute-start(bf16[2048,128]{1,0:T(8,128)(2,1)S(1)} %fusion.27), channel_id=1, source_target_pairs={{0,3},{1,0},{2,1},{3,2},{4,7},{5,4},{6,5},{7,6},{8,11},{9,8},{10,9... | collective-permute-start | bytes 1572872 | tf_op jit(solution)/shard_map/ppermute | solution.py:13
Sparse Core Ops, SparseCore 0:
  9.1 68.9 all-gather.1
  230.8 101.6 reduce-scatter.1

commit v4 on v3

--- a/solution.py
+++ b/solution.py
@@ -28,10 +28,11 @@
     )
     inner = jnp.arange(own_rows, dtype=jnp.int32)
     position = (packed_block[:, None] * own_rows + inner[None, :]).reshape(tokens)
-    query_position = (
-        packed_block.reshape(sections, cp_count).T.reshape(blocks)[:, None] * own_rows
-        + inner[None, :]
-    ).reshape(tokens)
+    y_count = cp_count // 4
+    query_order = (
+        packed_block.reshape(sections, y_count, 2, 2).transpose(3, 1, 2, 0).reshape(blocks)
+    )
+    query_position = (query_order[:, None] * own_rows + inner[None, :]).reshape(tokens)
     seq_ends = jnp.cumsum(lengths)
     sequence = jnp.sum((position[:, None] >= seq_ends[None, :]).astype(jnp.int32), axis=1)
     query_sequence = jnp.sum(
@@ -60,8 +61,8 @@
     one_head = (summed * inverse_rms[None, :, None]).astype(jnp.bfloat16)
     queries = (
         one_head[0]
-        .reshape(sections, cp_count, own_rows, HEAD)
-        .transpose(1, 0, 2, 3)
+        .reshape(sections, y_count, 2, 2, own_rows, HEAD)
+        .transpose(3, 1, 2, 0, 4, 5)
         .reshape(tokens, HEAD)
     )
     key_rows = one_head[1]
@@ -86,10 +87,44 @@
     partial_out = jnp.einsum(
         "kre,kew->rw", jnp.stack(parts), out_weight, preferred_element_type=jnp.float32
     ).astype(jnp.bfloat16)
-    reduced = lax.psum_scatter(partial_out, "cp", scatter_dimension=0, tiled=True)
-    branch = reduced.reshape(sections, own_rows, width_here)
-    return lax.all_to_all(branch, "section", split_axis=0, concat_axis=0, tiled=True)
+    me_cp = lax.axis_index("cp")
+    me_section = lax.axis_index("section")
+    me_core = me_cp % 2
+    me_y = me_cp // 4
+    me_z = me_cp // 2 % 2
+    staged = partial_out.reshape(2, y_count, 2, sections, own_rows, width_here)
+    kept = lax.dynamic_index_in_dim(staged, me_core, 0, keepdims=False)
+    given = lax.dynamic_index_in_dim(staged, 1 - me_core, 0, keepdims=False)
+    core_perm = [(c, c ^ 1) for c in range(cp_count)]
+    chip_sum = kept.astype(jnp.float32) + lax.ppermute(given, "cp", core_perm).astype(jnp.float32)
+    chip_half = chip_sum.astype(jnp.bfloat16)
+    y_sum = lax.dynamic_index_in_dim(chip_sum, me_y, 0, keepdims=False)
+    for step in range(1, y_count):
+        piece = lax.dynamic_index_in_dim(chip_half, (me_y + step) % y_count, 0, keepdims=False)
+        y_perm = [(c, ((c // 4 + step) % y_count) * 4 + c % 4) for c in range(cp_count)]
+        y_sum = y_sum + lax.ppermute(piece, "cp", y_perm).astype(jnp.float32)
+    y_half = y_sum.astype(jnp.bfloat16)
 
+    def piece_of(z_index, section_index):
+        z_part = lax.dynamic_index_in_dim(y_half, z_index, 0, keepdims=False)
+        return lax.dynamic_index_in_dim(z_part, section_index, 0, keepdims=False)
+
+    flat = sections * cp_count
+    z_flip = [(g, g // cp_count * cp_count + (g % cp_count ^ 2)) for g in range(flat)]
+    s_flip = [(g, (g + cp_count) % flat) for g in range(flat)]
+    both_flip = [(g, (g + cp_count) % flat // cp_count * cp_count + (g % cp_count ^ 2)) for g in range(flat)]
+    axes = ("section", "cp")
+    own_total = lax.dynamic_index_in_dim(
+        lax.dynamic_index_in_dim(y_sum, me_z, 0, keepdims=False), me_section, 0, keepdims=False
+    ) + lax.ppermute(piece_of(1 - me_z, me_section), axes, z_flip).astype(jnp.float32)
+    other_total = lax.ppermute(piece_of(me_z, 1 - me_section), axes, s_flip).astype(
+        jnp.float32
+    ) + lax.ppermute(piece_of(1 - me_z, 1 - me_section), axes, both_flip).astype(jnp.float32)
+    own_total = own_total.astype(jnp.bfloat16)
+    other_total = other_total.astype(jnp.bfloat16)
+    return jnp.where(
+        me_section == 0, jnp.stack([own_total, other_total]), jnp.stack([other_total, own_total])
+    )
 
 def solution(mesh):
     return jax.shard_map(

time: 351 us -> 330 us (0.940)
  waiting for transfers between devices: 243 us -> 203 us
  other arithmetic: 13.8 us -> 28.9 us
  blocking collectives: 10.7 us -> 0 us
  starting transfers between devices: 16.6 us -> 25.3 us
  local copies, waits for them, and re-layouts: 4.78 us -> 11.3 us
    reduce_scatter x1 -> x0, waiting for transfers between devices: 102 us -> none  [on_device(): lax.psum_scatter(partial_out, 'cp', scatter_dimension=0, tiled=True)]
    ppermute x0 -> x7, waiting for transfers between devices: none -> 61.9 us  [the longest x3 45.3 us: on_device(): y_sum = y_sum + lax.ppermute(piece, 'cp', y_perm).astype(jnp.float32)]
    convert_element_type x0 -> x2, other arithmetic: none -> 13.1 us  [the longest x1 8.81 us: on_device(): chip_half = chip_sum.astype(jnp.bfloat16)]
    all_to_all x1 -> x0, blocking collectives: 10.7 us -> none  [on_device(): lax.all_to_all(branch, 'section', split_axis=0, concat_axis=0, tiled=True)]
    ppermute x0 -> x7, starting transfers between devices: none -> 8.71 us  [the longest x3 4.54 us: on_device(): y_sum = y_sum + lax.ppermute(piece, 'cp', y_perm).astype(jnp.float32)]
    squeeze x0 -> x3, local copies, waits for them, and re-layouts: none -> 4.08 us  [the longest x1 2.26 us: on_device(): given = lax.dynamic_index_in_dim(staged, 1 - me_core, 0, keepdims=False)]
  transfers between devices with their start and end apart: 11 -> 17, of which waited for: 6 -> 12; matrix products, arithmetic and copies ran while one was open for 5% -> 6% of each run, Pallas kernels for 0% -> 0%
where the time goes in v4:
time: 330 us; the launch traced here: 329 us
  waiting for transfers between devices  203 us (62%)
  matrix products  46.4 us (14%)
  other arithmetic  28.9 us (9%)
  starting transfers between devices  25.3 us (8%)
  between operations  13.6 us (4%)
  local copies, waits for them, and re-layouts  11.3 us (3%)
    ppermute x9, waiting for transfers between devices, shifted(): lax.ppermute(value, axis, perm=[(j, (j + step) % count) for j in range(co...  70.5 us
    all_gather x1, waiting for transfers between devices, on_device(): lax.all_gather(rollout_rows, ('section', 'cp'), axis=0, tiled=True)  70 us
    ppermute x3, waiting for transfers between devices, on_device(): y_sum = y_sum + lax.ppermute(piece, 'cp', y_perm).astype(jnp.float32)  45.3 us
    dot_general x4, matrix products, head_partial(): jnp.einsum('rd,kde->kre', scaled, head_weights, preferred_element_type=jn...  27.2 us
    ppermute x9, starting transfers between devices, shifted(): lax.ppermute(value, axis, perm=[(j, (j + step) % count) for j in range(co...  16.5 us
    convert_element_type x1, other arithmetic, on_device(): chip_half = chip_sum.astype(jnp.bfloat16)  8.81 us
    ppermute x1, waiting for transfers between devices, on_device(): lax.ppermute(given, 'cp', core_perm).astype(jnp.float32)  7.5 us
    reduce_sum x1, other arithmetic, on_device(): row_total = jnp.sum(weights, axis=1, keepdims=True)  7.45 us
  transfers between devices with their start and end apart: 17, of which 12 were waited for; matrix products, arithmetic and copies ran while one was open for 6% of the time, Pallas kernels for 0%

profile of v4, /device:TPU:0, one launch (start us, length us, event | category | flops | bytes accessed | tf_op | source)
XLA Modules:
  0.0 328.6 jit_solution(13564220172805931652)
XLA Ops:
  6.5 0.7 all-gather.2.cloned.1.call-update
  7.3 0.8 select_reduce_fusion
  8.1 70.0 %all-gather.2.cloned.1.call-done = bf16[2048,2048]{1,0:T(8,128)(2,1)} async-done(((bf16[64,2048]{1,0:T(8,128)(2,1)}), bf16[2048,2048]{1,0:T(8,128)(2,1)}) %all-gather.2.cloned.1.call-update) | async-done | bytes 8388624 | tf_op jit(solution)/shard_map/all_gather | solution.py:24
  78.1 8.6 %fusion.12 = bf16[3,2048,128]{1,2,0:T(8,128)(2,1)} fusion(bf16[1,3,2048,512]{3,2,1,0:T(8,128)(2,1)} %param.10, s32[]{:T(128)S(6)} %select_n.163, bf16[2048,2048]{1,0:T(8,128)(2,1)} %all-gather.2.cloned.1.call-done, f32[2048]{0:T(1024)} %bitcast.111), kind=kOutput, calls=%fused_computation.24 | convolution fusion | flops 3234594816 | bytes 11542532 | tf_op jit(solution)/shard_map/rd,kde->kre/dot_general | solution.py:55
  86.6 1.5 collective-permute-start
  88.1 4.7 %fusion.13 = bf16[3,2048,128]{1,2,0:T(8,128)(2,1)} fusion(bf16[1,3,2048,512]{3,2,1,0:T(8,128)(2,1)S(1)} %copy-done.4, s32[]{:T(128)S(6)} %select_n.165, bf16[2048,2048]{1,0:T(8,128)(2,1)S(1)} %copy-done.1, f32[2048]{0:T(1024)S(1)} %bitcast.112), kind=kOutput, calls=%fused_computation.25 | convolution fusion | flops 3234594816 | bytes 11542532 | tf_op jit(solution)/shard_map/rd,kde->kre/dot_general | solution.py:55
  92.9 2.5 collective-permute-start.1
  95.4 4.7 %fusion.14 = bf16[3,2048,128]{1,2,0:T(8,128)(2,1)} fusion(bf16[1,3,2048,512]{3,2,1,0:T(8,128)(2,1)S(1)} %copy-done.4, s32[]{:T(128)S(6)} %select_n.167, bf16[2048,2048]{1,0:T(8,128)(2,1)S(1)} %copy-done.1, f32[2048]{0:T(1024)S(1)} %bitcast.113), kind=kOutput, calls=%fused_computation.26 | convolution fusion | flops 3234594816 | bytes 11542532 | tf_op jit(solution)/shard_map/rd,kde->kre/dot_general | solution.py:55
  100.1 1.6 collective-permute-start.2
  101.8 0.1 mul.54
  101.9 0.1 copy.19
  102.0 0.1 mul.56
  102.1 0.1 iota_add_fusion
  102.2 5.1 %fusion.1 = f32[2048]{0:T(1024)S(1)} fusion(bf16[2048,2048]{1,0:T(8,128)(2,1)} %all-gather.2.cloned.1.call-done), kind=kLoop, calls=%fused_computation.4 | loop fusion | flops 12580864 | bytes 8396800 | tf_op jit(solution)/shard_map/reduce_sum | solution.py:44
  107.3 0.5 collective-permute-start.3
  107.7 0.1 iota_add_fusion.1
  107.8 0.1 add.238
  107.9 0.1 add.242
  107.9 0.2 reduce-window.8
  108.1 1.1 collective-permute-start.4
  109.2 47.2 %collective-permute-done.3 = f32[2048]{0:T(1024)S(1)} collective-permute-done((f32[2048]{0:T(1024)S(1)}, f32[2048]{0:T(1024)S(1)}, u32[]{:S(2)}, u32[]{:S(2)}) %collective-permute-start.3) | collective-permute-done | bytes 8224 | tf_op jit(solution)/shard_map/ppermute | solution.py:13
  156.4 3.6 %collective-permute-start.5 = (f32[2048]{0:T(1024)S(1)}, f32[2048]{0:T(1024)S(1)}, u32[]{:S(2)}, u32[]{:S(2)}) collective-permute-start(f32[2048]{0:T(1024)S(1)} %fusion.1), channel_id=1, source_target_pairs={{0,3},{1,0},{2,1},{3,2},{4,7},{5,4},{6,5},{7,6},{8,11},{9,8},{10,9... | collective-permute-start | bytes 24584 | tf_op jit(solution)/shard_map/ppermute | solution.py:13
  160.0 0.1 fusion.49
  160.1 0.0 collective-permute-done.4
  160.1 3.8 %collective-permute-done.5 = f32[2048]{0:T(1024)S(1)} collective-permute-done((f32[2048]{0:T(1024)S(1)}, f32[2048]{0:T(1024)S(1)}, u32[]{:S(2)}, u32[]{:S(2)}) %collective-permute-start.5) | collective-permute-done | bytes 8224 | tf_op jit(solution)/shard_map/ppermute | solution.py:13
  163.9 0.0 collective-permute-done
  163.9 0.0 collective-permute-done.1
  163.9 0.0 collective-permute-done.2
  164.0 9.2 %fusion.11 = bf16[3,2048,128]{1,2,0:T(8,128)(2,1)S(1)} fusion(bf16[3,2048,128]{1,2,0:T(8,128)(2,1)} %collective-permute-done.2, bf16[3,2048,128]{1,2,0:T(8,128)(2,1)} %collective-permute-done.1, bf16[3,2048,128]{1,2,0:T(8,128)(2,1)} %collective-permute-done, f32[2048]{0:T(1024)S(1)} %add_rsqrt_fusion, bf16[1,3,2048,512]{3,2,1,0:T(8,128)(2,1)} %param.10, ...), kind=kOutput, calls=%fused_computation.20 | convolution fusion | flops 3240099840 | bytes 16269316 | tf_op jit(solution)/shard_map/rd,kde->kre/dot_general | solution.py:55
  173.2 1.1 copy-done.3
  174.3 0.3 copy.24
  174.7 5.7 %fusion.2 = (f32[2048]{0:T(1024)S(1)}, f32[2048,2048]{0,1:T(8,128)S(1)}) fusion(s32[2048]{0:T(1024)S(1)} %add.238, s32[2048]{0:T(1024)S(1)} %get-tuple-element.6, s32[2048]{0:T(1024)S(1)} %add.242, s32[2048]{0:T(1024)S(1)} %get-tuple-element.5, bf16[2048,128]{1,0:T(8,128)(2,1)S(1)} %bitcast.106, bf16[3,2048,128]{1,2,0:T(8,128)(2,1)} %copy-done.3), kind=kOutput, calls=%fused_computation.9 | convolution fusion | flops 1098905600 | bytes 17866752 | tf_op jit(solution)/shard_map/dot_general | solution.py:74
  180.4 7.4 %fusion.3 = f32[2048]{0:T(1024)S(1)} fusion(f32[2048,2048]{0,1:T(8,128)S(1)} %get-tuple-element.18, f32[2048]{0:T(1024)S(1)} %get-tuple-element.17, s32[2048]{0:T(1024)S(1)} %add.238, s32[2048]{0:T(1024)S(1)} %get-tuple-element.6, s32[2048]{0:T(1024)S(1)} %add.242, s32[2048]{0:T(1024)S(1)} %get-tuple-element.5), kind=kLoop, calls=%fused_computation.10 | loop fusion | flops 33552384 | bytes 16826368 | tf_op jit(solution)/shard_map/reduce_sum | solution.py:78
  187.9 7.0 %fusion.29 = bf16[2048,128]{1,0:T(8,128)(2,1)S(1)} fusion(f32[2048,2048]{0,1:T(8,128)S(1)} %get-tuple-element.18, f32[2048]{0:T(1024)S(1)} %get-tuple-element.17, s32[2048]{0:T(1024)S(1)} %add.238, s32[2048]{0:T(1024)S(1)} %get-tuple-element.6, s32[2048]{0:T(1024)S(1)} %add.242, s32[2048]{0:T(1024)S(1)} %get-tuple-element.5, ...), kind=kOutput, calls=%fused_computation.40 | convolution fusion | flops 1107820544 | bytes 17874944 | tf_op jit(solution)/shard_map/dot_general | solution.py:80
  194.9 2.5 collective-permute-start.6
  197.4 1.6 collective-permute-start.7
  199.1 1.6 collective-permute-start.8
  200.7 2.0 gather_fusion
  202.7 7.0 %collective-permute-done.6 = bf16[2048,128]{1,0:T(8,128)(2,1)S(1)} collective-permute-done((bf16[2048,128]{1,0:T(8,128)(2,1)S(1)}, bf16[2048,128]{1,0:T(8,128)(2,1)S(1)}, u32[]{:S(2)}, u32[]{:S(2)}) %collective-permute-start.6) | collective-permute-done | bytes 524320 | tf_op jit(solution)/shard_map/ppermute | solution.py:13
  209.7 12.5 %collective-permute-done.7 = bf16[2048,128]{1,0:T(8,128)(2,1)} collective-permute-done((bf16[2048,128]{1,0:T(8,128)(2,1)S(1)}, bf16[2048,128]{1,0:T(8,128)(2,1)}, u32[]{:S(2)}, u32[]{:S(2)}) %collective-permute-start.7) | collective-permute-done | bytes 524320 | tf_op jit(solution)/shard_map/ppermute | solution.py:13
  222.2 0.0 collective-permute-done.8
  222.2 6.4 %bitcast_convert_fusion = bf16[2048,2048]{1,0:T(8,128)(2,1)S(1)} fusion(bf16[1,2048,128]{2,1,0:T(8,128)(2,1)} %bitcast.21, bf16[1,2048,128]{2,1,0:T(8,128)(2,1)} %bitcast.20, bf16[1,2048,128]{2,1,0:T(8,128)(2,1)S(1)} %bitcast.110, bf16[1,2048,128]{2,1,0:T(8,128)(2,1)S(1)} %bitcast.109, bf16[4,128,2048]{2,1,0:T(8,128)(2,1)} %gather_fusion, ...), kind=kOutput, calls=%fused_computation.5 | convolution fusion | flops 4303355904 | bytes 12582916 | tf_op jit(solution)/shard_map/kre,kew->rw/dot_general | solution.py:87
  228.7 3.2 copy-done.2
  231.9 2.3 dynamic-slice_bitcast_fusion
  234.2 7.5 %collective-permute-done.9 = bf16[4,2,2,64,2048]{4,3,2,1,0:T(8,128)(2,1)} collective-permute-done((bf16[4,2,2,64,2048]{4,3,2,1,0:T(8,128)(2,1)}, bf16[4,2,2,64,2048]{4,3,2,1,0:T(8,128)(2,1)}, u32[]{:S(2)}, u32[]{:S(2)}) %collective-permute-start.9) | collective-permute-done | bytes 4194336 | tf_op jit(solution)/shard_map/ppermute | solution.py:99
  241.7 8.8 %fusion.68 = (bf16[4,2,2,64,2048]{4,3,2,1,0:T(8,128)(2,1)S(1)}, f32[4,2,2,64,2048]{4,3,2,1,0:T(8,128)}) fusion(bf16[4,2,2,64,2048]{4,3,2,1,0:T(8,128)(2,1)} %collective-permute-done.9, bf16[2,4,2,2,64,2048]{5,4,3,2,1,0:T(8,128)(2,1)} %bitcast.104, s32[]{:T(128)S(6)} %select_n.176), kind=kLoop, calls=%fused_computation.99 | loop fusion | flops 8388608 | bytes 20971524 | tf_op jit(solution)/shard_map/convert_element_type | solution.py:100
  250.5 1.7 dynamic-slice_bitcast_fusion.3
  252.2 1.2 collective-permute-start.10
  253.4 1.9 collective-permute-start.11
  255.3 1.4 collective-permute-start.12
  256.8 44.5 %collective-permute-done.10 = bf16[2,2,64,2048]{3,2,1,0:T(8,128)(2,1)S(1)} collective-permute-done((bf16[2,2,64,2048]{3,2,1,0:T(8,128)(2,1)}, bf16[2,2,64,2048]{3,2,1,0:T(8,128)(2,1)S(1)}, u32[]{:S(2)}, u32[]{:S(2)}) %collective-permute-start.10) | collective-permute-done | bytes 1048608 | tf_op jit(solution)/shard_map/ppermute | solution.py:105
  301.3 0.1 collective-permute-done.11
  301.4 0.6 collective-permute-done.12
  302.0 4.3 %fusion.66 = (bf16[2,2,64,2048]{3,2,1,0:T(8,128)(2,1)S(1)}, f32[2,2,64,2048]{3,2,1,0:T(8,128)}) fusion(bf16[2,2,64,2048]{3,2,1,0:T(8,128)(2,1)} %collective-permute-done.12, bf16[2,2,64,2048]{3,2,1,0:T(8,128)(2,1)} %collective-permute-done.11, bf16[2,2,64,2048]{3,2,1,0:T(8,128)(2,1)S(1)} %collective-permute-done.10, ...), kind=kLoop, calls=%fused_computation.98 | loop fusion | flops 3670016 | bytes 8388612 | tf_op jit(solution)/shard_map/convert_element_type | solution.py:106
  306.3 0.1 dynamic-slice_bitcast_fusion.6
  306.4 2.2 collective-permute-start.13
  308.6 0.6 collective-permute-start.14
  309.1 1.4 collective-permute-start.15
  310.6 6.7 %collective-permute-done.13 = bf16[64,2048]{1,0:T(8,128)(2,1)S(1)} collective-permute-done((bf16[64,2048]{1,0:T(8,128)(2,1)S(1)}, bf16[64,2048]{1,0:T(8,128)(2,1)S(1)}, u32[]{:S(2)}, u32[]{:S(2)}) %collective-permute-start.13) | collective-permute-done | bytes 262176 | tf_op jit(solution)/shard_map/ppermute | solution.py:119
  317.2 1.1 fusion.47
  318.3 1.6 collective-permute-done.14
  320.0 0.8 collective-permute-done.15
  320.8 0.1 fusion.46
  320.8 0.9 maximum_select_fusion
  (21 shorter events, 0.2 us)
Async XLA Ops:
  6.5 194.2 %copy-start = (bf16[1,512,2048]{2,1,0:T(8,128)(2,1)S(1)}, bf16[1,512,2048]{2,1,0:T(8,128)(2,1)}, u32[]{:S(2)}) copy-start(bf16[1,512,2048]{2,1,0:T(8,128)(2,1)} %param.11) | copy-start | bytes 6291460
  6.5 71.5 %all-gather.2.cloned.1.call-start = ((), (), s32[]{:S(2)}) async-start(), calls=%async_computation | async-start | bytes 8650752 | tf_op jit(solution)/shard_map/all_gather | solution.py:24
  78.1 10.0 %copy-start.1 = (bf16[2048,2048]{1,0:T(8,128)(2,1)S(1)}, bf16[2048,2048]{1,0:T(8,128)(2,1)}, u32[]{:S(2)}) copy-start(bf16[2048,2048]{1,0:T(8,128)(2,1)} %all-gather.2.cloned.1.call-done) | copy-start | bytes 25165828
  78.1 10.0 %copy-start.4 = (bf16[1,3,2048,512]{3,2,1,0:T(8,128)(2,1)S(1)}, bf16[1,3,2048,512]{3,2,1,0:T(8,128)(2,1)}, u32[]{:S(2)}) copy-start(bf16[1,3,2048,512]{3,2,1,0:T(8,128)(2,1)} %param.10) | copy-start | bytes 18874372
  78.1 10.0 %copy-start.5 = (f32[1,2048]{1,0:T(1,128)S(1)}, f32[1,2048]{1,0:T(1,128)}, u32[]{:S(2)}) copy-start(f32[1,2048]{1,0:T(1,128)} %param.9) | copy-start | bytes 24580
  86.6 77.3 %collective-permute-start = (bf16[3,2048,128]{1,2,0:T(8,128)(2,1)}, bf16[3,2048,128]{1,2,0:T(8,128)(2,1)}, u32[]{:S(2)}, u32[]{:S(2)}) collective-permute-start(bf16[3,2048,128]{1,2,0:T(8,128)(2,1)} %fusion.12), channel_id=1, source_target_pairs={{0,1},{1,2},{2,3},{3,0},{4,5},{5,6},{6,7},{7,4},{8,9},{9,10},{10,1... | collective-permute-start | bytes 4718600 | tf_op jit(solution)/shard_map/ppermute | solution.py:13
  92.9 71.1 %collective-permute-start.1 = (bf16[3,2048,128]{1,2,0:T(8,128)(2,1)}, bf16[3,2048,128]{1,2,0:T(8,128)(2,1)}, u32[]{:S(2)}, u32[]{:S(2)}) collective-permute-start(bf16[3,2048,128]{1,2,0:T(8,128)(2,1)} %fusion.13), channel_id=1, source_target_pairs={{0,2},{1,3},{2,0},{3,1},{4,6},{5,7},{6,4},{7,5},{8,10},{9,11},{10,... | collective-permute-start | bytes 4718600 | tf_op jit(solution)/shard_map/ppermute | solution.py:13
  100.1 7.8 %copy-start.6 = (s32[2]{0:T(128)S(1)}, s32[2]{0:T(128)}, u32[]{:S(2)}) copy-start(s32[2]{0:T(128)} %param.7) | copy-start | bytes 28
  100.1 63.8 %collective-permute-start.2 = (bf16[3,2048,128]{1,2,0:T(8,128)(2,1)}, bf16[3,2048,128]{1,2,0:T(8,128)(2,1)}, u32[]{:S(2)}, u32[]{:S(2)}) collective-permute-start(bf16[3,2048,128]{1,2,0:T(8,128)(2,1)} %fusion.14), channel_id=1, source_target_pairs={{0,3},{1,0},{2,1},{3,2},{4,7},{5,4},{6,5},{7,6},{8,11},{9,8},{10,9... | collective-permute-start | bytes 4718600 | tf_op jit(solution)/shard_map/ppermute | solution.py:13
  107.3 49.2 %collective-permute-start.3 = (f32[2048]{0:T(1024)S(1)}, f32[2048]{0:T(1024)S(1)}, u32[]{:S(2)}, u32[]{:S(2)}) collective-permute-start(f32[2048]{0:T(1024)S(1)} %fusion.1), channel_id=1, source_target_pairs={{0,1},{1,2},{2,3},{3,0},{4,5},{5,6},{6,7},{7,4},{8,9},{9,10},{10,1... | collective-permute-start | bytes 24584 | tf_op jit(solution)/shard_map/ppermute | solution.py:13
  108.1 52.0 %collective-permute-start.4 = (f32[2048]{0:T(1024)S(1)}, f32[2048]{0:T(1024)S(1)}, u32[]{:S(2)}, u32[]{:S(2)}) collective-permute-start(f32[2048]{0:T(1024)S(1)} %fusion.1), channel_id=1, source_target_pairs={{0,2},{1,3},{2,0},{3,1},{4,6},{5,7},{6,4},{7,5},{8,10},{9,11},{10,... | collective-permute-start | bytes 24584 | tf_op jit(solution)/shard_map/ppermute | solution.py:13
  156.4 7.5 %collective-permute-start.5 = (f32[2048]{0:T(1024)S(1)}, f32[2048]{0:T(1024)S(1)}, u32[]{:S(2)}, u32[]{:S(2)}) collective-permute-start(f32[2048]{0:T(1024)S(1)} %fusion.1), channel_id=1, source_target_pairs={{0,3},{1,0},{2,1},{3,2},{4,7},{5,4},{6,5},{7,6},{8,11},{9,8},{10,9... | collective-permute-start | bytes 24584 | tf_op jit(solution)/shard_map/ppermute | solution.py:13
  173.2 1.2 copy-start.3
  194.9 14.8 %collective-permute-start.6 = (bf16[2048,128]{1,0:T(8,128)(2,1)S(1)}, bf16[2048,128]{1,0:T(8,128)(2,1)S(1)}, u32[]{:S(2)}, u32[]{:S(2)}) collective-permute-start(bf16[2048,128]{1,0:T(8,128)(2,1)S(1)} %fusion.29), channel_id=1, source_target_pairs={{0,1},{1,2},{2,3},{3,0},{4,5},{5,6},{6,7},{7,4},{8,9},{9,10},{10,1... | collective-permute-start | bytes 1572872 | tf_op jit(solution)/shard_map/ppermute | solution.py:13
  197.4 24.8 %collective-permute-start.7 = (bf16[2048,128]{1,0:T(8,128)(2,1)S(1)}, bf16[2048,128]{1,0:T(8,128)(2,1)}, u32[]{:S(2)}, u32[]{:S(2)}) collective-permute-start(bf16[2048,128]{1,0:T(8,128)(2,1)S(1)} %fusion.29), channel_id=1, source_target_pairs={{0,2},{1,3},{2,0},{3,1},{4,6},{5,7},{6,4},{7,5},{8,10},{9,11},{10,... | collective-permute-start | bytes 1572872 | tf_op jit(solution)/shard_map/ppermute | solution.py:13
  199.1 23.2 %collective-permute-start.8 = (bf16[2048,128]{1,0:T(8,128)(2,1)S(1)}, bf16[2048,128]{1,0:T(8,128)(2,1)}, u32[]{:S(2)}, u32[]{:S(2)}) collective-permute-start(bf16[2048,128]{1,0:T(8,128)(2,1)S(1)} %fusion.29), channel_id=1, source_target_pairs={{0,3},{1,0},{2,1},{3,2},{4,7},{5,4},{6,5},{7,6},{8,11},{9,8},{10,9... | collective-permute-start | bytes 1572872 | tf_op jit(solution)/shard_map/ppermute | solution.py:13
  228.7 3.2 copy-start.2
  234.2 7.5 %collective-permute-start.9 = (bf16[4,2,2,64,2048]{4,3,2,1,0:T(8,128)(2,1)}, bf16[4,2,2,64,2048]{4,3,2,1,0:T(8,128)(2,1)}, u32[]{:S(2)}, u32[]{:S(2)}) collective-permute-start(bf16[4,2,2,64,2048]{4,3,2,1,0:T(8,128)(2,1)} %dynamic-slice_bitcast_fusion), channel_id=1, source_target_pairs={{0,4},{4,0},{8,12},{12,8},{16,20},{20,16},{24,28},{28,24},{32,36},... | collective-permute-start | bytes 12582920 | tf_op jit(solution)/shard_map/ppermute | solution.py:99
  252.2 49.1 %collective-permute-start.10 = (bf16[2,2,64,2048]{3,2,1,0:T(8,128)(2,1)}, bf16[2,2,64,2048]{3,2,1,0:T(8,128)(2,1)S(1)}, u32[]{:S(2)}, u32[]{:S(2)}) collective-permute-start(bf16[2,2,64,2048]{3,2,1,0:T(8,128)(2,1)} %get-tuple-element.11), channel_id=1, source_target_pairs={{0,16},{4,20},{8,24},{12,28},{16,32},{20,36},{24,40},{28,44},{32,4... | collective-permute-start | bytes 3145736 | tf_op jit(solution)/shard_map/ppermute | solution.py:105
  253.4 48.0 %collective-permute-start.11 = (bf16[2,2,64,2048]{3,2,1,0:T(8,128)(2,1)}, bf16[2,2,64,2048]{3,2,1,0:T(8,128)(2,1)}, u32[]{:S(2)}, u32[]{:S(2)}) collective-permute-start(bf16[2,2,64,2048]{3,2,1,0:T(8,128)(2,1)} %get-tuple-element.13), channel_id=1, source_target_pairs={{0,32},{4,36},{8,40},{12,44},{16,48},{20,52},{24,56},{28,60},{32,0... | collective-permute-start | bytes 3145736 | tf_op jit(solution)/shard_map/ppermute | solution.py:105
  255.3 46.7 %collective-permute-start.12 = (bf16[2,2,64,2048]{3,2,1,0:T(8,128)(2,1)}, bf16[2,2,64,2048]{3,2,1,0:T(8,128)(2,1)}, u32[]{:S(2)}, u32[]{:S(2)}) collective-permute-start(bf16[2,2,64,2048]{3,2,1,0:T(8,128)(2,1)} %get-tuple-element.12), channel_id=1, source_target_pairs={{0,48},{4,52},{8,56},{12,60},{16,0},{20,4},{24,8},{28,12},{32,16},... | collective-permute-start | bytes 3145736 | tf_op jit(solution)/shard_map/ppermute | solution.py:105
  306.4 10.9 %collective-permute-start.13 = (bf16[64,2048]{1,0:T(8,128)(2,1)S(1)}, bf16[64,2048]{1,0:T(8,128)(2,1)S(1)}, u32[]{:S(2)}, u32[]{:S(2)}) collective-permute-start(bf16[64,2048]{1,0:T(8,128)(2,1)S(1)} %get-tuple-element.14), channel_id=1, source_target_pairs={{0,8},{4,12},{8,0},{12,4},{16,24},{20,28},{24,16},{28,20},{32,40},... | collective-permute-start | bytes 786440 | tf_op jit(solution)/shard_map/ppermute | solution.py:119
  308.6 11.4 %collective-permute-start.14 = (bf16[64,2048]{1,0:T(8,128)(2,1)S(1)}, bf16[64,2048]{1,0:T(8,128)(2,1)S(1)}, u32[]{:S(2)}, u32[]{:S(2)}) collective-permute-start(bf16[64,2048]{1,0:T(8,128)(2,1)S(1)} %get-tuple-element.16), channel_id=1, source_target_pairs={{0,64},{4,68},{8,72},{12,76},{16,80},{20,84},{24,88},{28,92},{32,9... | collective-permute-start | bytes 786440 | tf_op jit(solution)/shard_map/ppermute | solution.py:120
  309.1 11.6 %collective-permute-start.15 = (bf16[64,2048]{1,0:T(8,128)(2,1)S(1)}, bf16[64,2048]{1,0:T(8,128)(2,1)S(1)}, u32[]{:S(2)}, u32[]{:S(2)}) collective-permute-start(bf16[64,2048]{1,0:T(8,128)(2,1)S(1)} %get-tuple-element.15), channel_id=1, source_target_pairs={{0,72},{4,76},{8,64},{12,68},{16,88},{20,92},{24,80},{28,84},{32,1... | collective-permute-start | bytes 786440 | tf_op jit(solution)/shard_map/ppermute | solution.py:122
Sparse Core Ops, SparseCore 0:
  9.1 68.9 all-gather.1
